TPU v7x, 32 devices: a whole 2x2x4 slice. The times are simulated.
32 devices in a mesh: groups: 2 (over y), user: 8 (over z, x), item: 2 (over core).
Axes of the slice: x: 2, y: 2, z: 4, core: 2. Of those that a mesh axis runs over, the one named last changes fastest.
Arguments:
- user_factors: float32 [49152, 256], P(('groups', 'user')), parts along dimension 0, may hold values from -1.5 to 1.5
- item_factors: float32 [16384, 256], P(('groups', 'user', 'item')), parts along dimension 0, may hold values from -1.5 to 1.5
- stratum_masks: int32 [4], P('groups'), parts along dimension 0, may hold values from 1 to 7
- block_codes: int32 [16, 2, 128], P(('groups', 'user'), 'item'), parts along dimension 0, may hold values from 0 to 95, as said below
- block_counts: int32 [16, 2, 2], P(('groups', 'user'), 'item'), parts along dimension 0, may hold values from 1 to 64
- ratings: bfloat16 [16, 2, 128, 128, 128], P(('groups', 'user'), 'item'), parts along dimension 0, may hold values from -6 to 6
Outputs:
- user_out: float32 [49152, 256], P(('groups', 'user')), parts along dimension 0
- item_out: float32 [16384, 256], P(('groups', 'user', 'item')), parts along dimension 0
There are 2 independent parts, one for each index of `groups`. A program takes and returns all parts, laid end to end along the dimension named above; each array names one. Nothing has to cross between parts.
Inputs may be any that keep to these rules, and one draw needn't show every extreme that they name: `stratum_masks`: each mask m pairs user index u with user index u XOR m. `block_codes`: within one device and stratum the 64 codes are distinct.
All inputs are finite; a program needn't handle non-finite values.
Results may differ from a plain program's by a relative error of at most 0.0011.
Values sent between devices are 32-bit elements; how exact they have to be, the bound alone decides.
No kernel may reach another device: no remote copies, remote signals or barrier semaphores. Data moves between devices by JAX's collectives and lax.ppermute only.
A program may use at most 128 MiB of HBM per device.

v0:
```python
import jax
import jax.numpy as jnp
from jax import lax
from jax.sharding import PartitionSpec as P

LEARNING_RATE = 0.02
WEIGHT_DECAY = 0.1


def moved(value, partner_mask):
    count = lax.axis_size("user")

    def branch(mask):
        if mask == 0:
            return lambda held: held
        pairs = [(source, source ^ mask) for source in range(count)]
        return lambda held: lax.ppermute(held, "user", pairs)

    return lax.switch(partner_mask, [branch(mask) for mask in range(count)], value)


def item_sum(value):
    if lax.axis_size("item") == 2:
        return value + lax.ppermute(value, "item", [(0, 1), (1, 0)])
    return lax.psum(value, "item")


def local_grads(user_rows, panel_rows, codes, count, blocks):
    tile_size = blocks.shape[-1]
    user_tiles = user_rows.shape[0] // tile_size
    item_tiles = panel_rows.shape[0] // tile_size
    code_count = user_tiles * item_tiles
    slot_count = codes.shape[0]
    user_bf = user_rows.astype(jnp.bfloat16)
    panel_bf = panel_rows.astype(jnp.bfloat16)
    hits = (codes[:, None] == lax.iota(jnp.int32, code_count)[None, :]) & (
        lax.iota(jnp.int32, slot_count) < count
    )[:, None]
    live = jnp.any(hits, axis=0)
    slot_of = jnp.sum(jnp.where(hits, lax.iota(jnp.int32, slot_count)[:, None], 0), axis=0)
    dense = jnp.take(blocks, slot_of, axis=0).reshape(user_tiles, item_tiles, tile_size, tile_size)
    dense = dense.transpose(0, 2, 1, 3).reshape(user_tiles * tile_size, item_tiles * tile_size)
    live_dense = jnp.broadcast_to(
        live.reshape(user_tiles, 1, item_tiles, 1).astype(jnp.float32),
        (user_tiles, tile_size, item_tiles, tile_size),
    ).reshape(user_tiles * tile_size, item_tiles * tile_size)
    scores = lax.dot_general(
        user_bf, panel_bf, (((1,), (1,)), ((), ())), preferred_element_type=jnp.float32
    )
    errors = ((scores - dense.astype(jnp.float32)) * live_dense).astype(jnp.bfloat16)
    grad_user = lax.dot_general(
        errors, panel_bf, (((1,), (0,)), ((), ())), preferred_element_type=jnp.float32
    )
    grad_panel = lax.dot_general(
        errors, user_bf, (((0,), (0,)), ((), ())), preferred_element_type=jnp.float32
    )
    return grad_user, grad_panel


def local(user_factors, item_factors, stratum_masks, block_codes, block_counts, ratings):
    stratum_total = stratum_masks.shape[0]
    slot_count = block_codes.shape[-1] // stratum_total

    user_rows = user_factors
    panel_now = moved(item_factors, stratum_masks[0])
    for stratum in range(stratum_total):
        codes = block_codes[0, 0, stratum * slot_count : (stratum + 1) * slot_count]
        count = block_counts[0, 0, stratum]
        blocks = ratings[0, 0, stratum * slot_count : (stratum + 1) * slot_count]
        grad_user, grad_panel = local_grads(user_rows, panel_now, codes, count, blocks)
        panel_next = panel_now - LEARNING_RATE * (grad_panel + WEIGHT_DECAY * panel_now)
        if stratum + 1 < stratum_total:
            step_mask = jnp.bitwise_xor(stratum_masks[stratum], stratum_masks[stratum + 1])
        else:
            step_mask = stratum_masks[stratum]
        panel_now = moved(panel_next, step_mask)
        grad_total = item_sum(grad_user)
        user_rows = user_rows - LEARNING_RATE * (grad_total + WEIGHT_DECAY * user_rows)
    return (user_rows, panel_now)


def solution(mesh):
    placed = (
        P(("groups", "user"), None),
        P(("groups", "user", "item"), None),
        P("groups"),
        P(("groups", "user"), "item", None),
        P(("groups", "user"), "item", None),
        P(("groups", "user"), "item", None, None, None),
    )
    return jax.shard_map(
        local,
        mesh=mesh,
        in_specs=placed,
        out_specs=(P(("groups", "user"), None), P(("groups", "user", "item"), None)),
        check_vma=False,
    )
```

profile of v0, /device:TPU:0, one launch (start us, length us, event | category | flops | bytes accessed | tf_op | source)
XLA Modules:
  0.0 142.0 jit_solution(908428812803746187)
XLA Ops:
  0.6 1.3 fusion.20
  1.9 0.6 iota_compare_fusion.2
  2.6 0.7 iota_compare_fusion.3
  3.3 0.8 slice_bitcast_fusion.2
  4.3 4.0 %slice_bitcast_fusion = (bf16[64,128,128]{2,1,0:T(8,128)(2,1)S(1)}, bf16[64,128,128]{2,1,0:T(8,128)(2,1)}) fusion(bf16[1,1,128,128,128]{4,3,2,1,0:T(8,128)(2,1)} %param.37), kind=kLoop, calls=%fused_computation.20 | loop fusion | bytes 8388608 | tf_op jit(solution)/shard_map/squeeze | solution.py:69
  8.3 4.3 %gather_fusion = bf16[96,128,128]{2,1,0:T(8,128)(2,1)} fusion(bf16[64,128,128]{2,1,0:T(8,128)(2,1)} %get-tuple-element.190, s32[1024]{0:T(1024)S(1)} %pad_clamp_fusion.1), kind=kCustom, calls=%fused_computation.clone | custom fusion | bytes 6291840 | tf_op jit(solution)/shard_map/jit(_take)/gather | solution.py:41
  12.6 3.9 %broadcast_select_fusion.1 = bf16[96,128,128]{2,1,0:T(8,128)(2,1)} fusion(bf16[96,128,128]{2,1,0:T(8,128)(2,1)} %gather_fusion, pred[96]{0:T(512)(128)(4,1)S(1)} %compare_and_fusion.1), kind=kLoop, calls=%fused_computation.19 | loop fusion | flops 1572864 | bytes 6291552 | tf_op jit(solution)/shard_map/jit(_take)/select_n | solution.py:41
  16.6 5.5 %copy.14 = f32[24,4,128,128]{2,0,3,1:T(8,128)} copy(bf16[24,4,128,128]{3,2,1,0:T(8,128)(2,1)} %bitcast.57) | data formatting | bytes 9437184 | tf_op jit(solution)/shard_map/convert_element_type | solution.py:50
  23.5 17.2 %conditional.5 = (f32[512,256]{1,0:T(8,128)S(1)}) conditional(s32[]{:T(128)} %bitcast, f32[512,256]{1,0:T(8,128)S(1)} %copy-done, f32[512,256]{1,0:T(8,128)S(1)} %copy-done, f32[512,256]{1,0:T(8,128)S(1)} %copy-done, f32[512,256]{1,0:T(8,128)S(1)} %copy-done, f32[512,256]{1,0:T(8,128)S(1)} %copy-done, ...), branch_computations={%region_0.0_spmd, %region_1.0_spmd, %region_2.0_spmd, %region_3.0_... | conditional | bytes 3145776 | solution.py:19
  23.5 5.1 %collective-permute-start.5 = (f32[512,256]{1,0:T(8,128)S(1)}, f32[512,256]{1,0:T(8,128)S(1)}, u32[]{:S(2)}, u32[]{:S(2)}) collective-permute-start(f32[512,256]{1,0:T(8,128)S(1)} %param.6), channel_id=1, source_target_pairs={{0,12},{2,14},{4,8},{6,10},{8,4},{10,6},{12,0},{14,2},{1,13},{3,15... | collective-permute-start | bytes 1572872 | tf_op jit(solution)/shard_map/cond/branch_6_fun/ppermute | solution.py:17
  28.7 12.0 %collective-permute-done.5 = f32[512,256]{1,0:T(8,128)S(1)} collective-permute-done((f32[512,256]{1,0:T(8,128)S(1)}, f32[512,256]{1,0:T(8,128)S(1)}, u32[]{:S(2)}, u32[]{:S(2)}) %collective-permute-start.5) | collective-permute-done | bytes 524320 | tf_op jit(solution)/shard_map/cond/branch_6_fun/ppermute | solution.py:17
  41.2 1.4 copy-done.2
  42.6 5.2 %fusion.1 = bf16[3072,512]{0,1:T(8,128)(2,1)S(1)} fusion(f32[64,8,24,128]{3,2,1,0:T(8,128)S(1)} %bitcast.55, f32[64,8,24,128]{3,2,1,0:T(8,128)} %bitcast.54, f32[3072,256]{1,0:T(8,128)S(1)} %copy-done.2, f32[512,256]{1,0:T(8,128)S(1)} %get-tuple-element.233), kind=kOutput, calls=%fused_computation.14 | convolution fusion | flops 810942464 | bytes 19398656 | tf_op jit(solution)/shard_map/dot_general | solution.py:47
  47.8 2.7 %fusion.12 = f32[3072,256]{1,0:T(8,128)} fusion(bf16[3072,512]{0,1:T(8,128)(2,1)S(1)} %fusion.1, f32[512,256]{1,0:T(8,128)S(1)} %get-tuple-element.233), kind=kOutput, calls=%fused_computation.33 | convolution fusion | flops 805437440 | bytes 6815744 | tf_op jit(solution)/shard_map/dot_general | solution.py:51
  51.8 2.7 %gather_fusion.1 = bf16[96,128,128]{2,1,0:T(8,128)(2,1)} fusion(bf16[64,128,128]{2,1,0:T(8,128)(2,1)S(1)} %get-tuple-element.189, s32[1024]{0:T(1024)S(1)} %pad_clamp_fusion), kind=kCustom, calls=%fused_computation.1.clone | custom fusion | bytes 6291840 | tf_op jit(solution)/shard_map/jit(_take)/gather | solution.py:41
  54.5 2.2 %broadcast_select_fusion = bf16[96,128,128]{2,1,0:T(8,128)(2,1)S(1)} fusion(bf16[96,128,128]{2,1,0:T(8,128)(2,1)} %gather_fusion.1, pred[96]{0:T(512)(128)(4,1)S(1)} %compare_and_fusion), kind=kLoop, calls=%fused_computation.18 | loop fusion | flops 1572864 | bytes 6291552 | tf_op jit(solution)/shard_map/jit(_take)/select_n | solution.py:41
  56.7 5.6 %copy.16 = f32[24,4,128,128]{3,1,2,0:T(4,128)} copy(bf16[24,4,128,128]{3,2,1,0:T(8,128)(2,1)S(1)} %bitcast.58) | data formatting | bytes 9437184 | tf_op jit(solution)/shard_map/convert_element_type | solution.py:50
  62.4 3.8 %fusion.6 = f32[512,256]{1,0:T(8,128)S(1)} fusion(bf16[3072,512]{0,1:T(8,128)(2,1)} %copy-done.1, f32[3072,256]{1,0:T(8,128)} %param.32), kind=kOutput, calls=%fused_computation.27 | convolution fusion | flops 806092800 | bytes 6815744 | tf_op jit(solution)/shard_map/dot_general | solution.py:54
  66.3 38.2 %conditional.8 = (f32[512,256]{1,0:T(8,128)}, f32[512,256]{1,0:T(8,128)S(1)}) conditional(s32[]{:T(128)} %bitcast.7, (f32[512,256]{1,0:T(8,128)S(1)}, f32[512,256]{1,0:T(8,128)S(1)}, f32[512,256]{1,0:T(8,128)S(1)}) %tuple.165, (f32[512,256]{1,0:T(8,128)S(1)}, f32[512,256]{1,0:T(8,128)S(1)}, ...), branch_computations={%region_10.12_spmd, %region_11.13_spmd, %region_12.14_spmd, %regio... | conditional | flops 524288 | bytes 5242936
  66.6 12.9 %collective-permute-start.18 = (f32[512,256]{1,0:T(8,128)S(1)}, f32[512,256]{1,0:T(8,128)}, u32[]{:S(2)}, u32[]{:S(2)}) collective-permute-start(f32[512,256]{1,0:T(8,128)S(1)} %multiply_subtract_fusion.5), channel_id=1, source_target_pairs={{0,10},{2,8},{4,14},{6,12},{8,2},{10,0},{12,6},{14,4},{1,11},{3,9}... | collective-permute-start | bytes 1572872 | tf_op jit(solution)/shard_map/cond/branch_5_fun/ppermute | solution.py:17
  79.5 23.9 %collective-permute-done.18 = f32[512,256]{1,0:T(8,128)} collective-permute-done((f32[512,256]{1,0:T(8,128)S(1)}, f32[512,256]{1,0:T(8,128)}, u32[]{:S(2)}, u32[]{:S(2)}) %collective-permute-start.18) | collective-permute-done | bytes 524320 | tf_op jit(solution)/shard_map/cond/branch_5_fun/ppermute | solution.py:17
  103.4 1.0 copy.63
  104.5 0.8 copy-done.3
  105.3 4.4 %multiply_subtract_fusion.9 = f32[3072,256]{1,0:T(8,128)S(1)} fusion(f32[3072,256]{1,0:T(8,128)} %param.32, f32[3072,256]{1,0:T(8,128)} %fusion.12, f32[3072,256]{1,0:T(8,128)} %collective-permute-done.21), kind=kLoop, calls=%fused_computation.17 | loop fusion | flops 3932160 | bytes 12582912 | tf_op jit(solution)/shard_map/sub | solution.py:78
  109.7 0.9 broadcast_in_dim.47
  110.7 3.8 %fusion = bf16[3072,512]{1,0:T(8,128)(2,1)S(1)} fusion(f32[384,8,4,128]{3,2,1,0:T(4,128)S(1)} %bitcast.56, f32[384,8,4,128]{3,2,1,0:T(4,128)} %bitcast.53, f32[3072,256]{1,0:T(8,128)S(1)} %multiply_subtract_fusion.9, f32[512,256]{1,0:T(8,128)S(1)} %copy-done.4), kind=kOutput, calls=%fused_computation.11 | convolution fusion | flops 810942464 | bytes 19398656 | tf_op jit(solution)/shard_map/dot_general | solution.py:47
  114.5 2.6 %fusion.10 = f32[3072,256]{1,0:T(8,128)} fusion(bf16[3072,512]{1,0:T(8,128)(2,1)S(1)} %fusion, f32[512,256]{1,0:T(8,128)S(1)} %copy-done.4), kind=kOutput, calls=%fused_computation.31 | convolution fusion | flops 805437440 | bytes 6815744 | tf_op jit(solution)/shard_map/dot_general | solution.py:51
  117.7 2.9 %fusion.3 = f32[512,256]{1,0:T(8,128)} fusion(f32[512,256]{1,0:T(8,128)} %get-tuple-element.184, bf16[3072,512]{1,0:T(8,128)(2,1)S(1)} %fusion, f32[3072,256]{1,0:T(8,128)S(1)} %multiply_subtract_fusion.9), kind=kOutput, calls=%fused_computation.24 | convolution fusion | flops 806617088 | bytes 7340032 | tf_op jit(solution)/shard_map/dot_general | solution.py:54
  120.6 16.2 %conditional.7 = (f32[512,256]{1,0:T(8,128)}) conditional(s32[]{:T(128)} %bitcast.13, f32[512,256]{1,0:T(8,128)} %fusion.3, f32[512,256]{1,0:T(8,128)} %fusion.3, f32[512,256]{1,0:T(8,128)} %fusion.3, f32[512,256]{1,0:T(8,128)} %fusion.3, f32[512,256]{1,0:T(8,128)} %fusion.3, f32[512,256]{1,0:T(8,128)} %fusion.3, ...), branch_computations={%region_20.22_spmd, %region_21.23_spmd, %region_22.24_spmd, %regio... | conditional | bytes 3145776 | solution.py:19
  120.6 15.4 %collective-permute-done.9 = f32[512,256]{1,0:T(8,128)S(1)} collective-permute-done((f32[512,256]{1,0:T(8,128)}, f32[512,256]{1,0:T(8,128)S(1)}, u32[]{:S(2)}, u32[]{:S(2)}) %collective-permute-start.9) | collective-permute-done | bytes 524320 | tf_op jit(solution)/shard_map/cond/branch_3_fun/ppermute | solution.py:17
  136.1 0.8 copy.52
  136.9 5.1 %multiply_subtract_fusion.8 = f32[3072,256]{1,0:T(8,128)} fusion(f32[3072,256]{1,0:T(8,128)S(1)} %multiply_subtract_fusion.9, f32[3072,256]{1,0:T(8,128)} %fusion.10, f32[3072,256]{1,0:T(8,128)} %collective-permute-done.22), kind=kLoop, calls=%fused_computation.16 | loop fusion | flops 3932160 | bytes 12582912 | tf_op jit(solution)/shard_map/sub | solution.py:78
  (33 shorter events, 2.0 us)
Async XLA Ops:
  16.5 5.7 %copy-start.5 = (s32[2]{0:T(128)S(1)}, s32[2]{0:T(128)}, u32[]{:S(2)}) copy-start(s32[2]{0:T(128)} %param.34) | copy-start | bytes 28
  16.6 6.9 %copy-start = (f32[512,256]{1,0:T(8,128)S(1)}, f32[512,256]{1,0:T(8,128)}, u32[]{:S(2)}) copy-start(f32[512,256]{1,0:T(8,128)} %param.33) | copy-start | bytes 1572868
  23.5 17.1 %collective-permute-start.5 = (f32[512,256]{1,0:T(8,128)S(1)}, f32[512,256]{1,0:T(8,128)S(1)}, u32[]{:S(2)}, u32[]{:S(2)}) collective-permute-start(f32[512,256]{1,0:T(8,128)S(1)} %param.6), channel_id=1, source_target_pairs={{0,12},{2,14},{4,8},{6,10},{8,4},{10,6},{12,0},{14,2},{1,13},{3,15... | collective-permute-start | bytes 1572872 | tf_op jit(solution)/shard_map/cond/branch_6_fun/ppermute | solution.py:17
  40.7 1.9 %copy-start.2 = (f32[3072,256]{1,0:T(8,128)S(1)}, f32[3072,256]{1,0:T(8,128)}, u32[]{:S(2)}) copy-start(f32[3072,256]{1,0:T(8,128)} %param.32) | copy-start | bytes 9437188
  47.8 2.7 %copy-start.1 = (bf16[3072,512]{0,1:T(8,128)(2,1)}, bf16[3072,512]{0,1:T(8,128)(2,1)S(1)}, u32[]{:S(2)}) copy-start(bf16[3072,512]{0,1:T(8,128)(2,1)S(1)} %fusion.1) | copy-start | bytes 9437188
  50.5 54.7 %collective-permute-start.21 = (f32[3072,256]{1,0:T(8,128)}, f32[3072,256]{1,0:T(8,128)}, u32[]{:S(2)}, u32[]{:S(2)}) collective-permute-start(f32[3072,256]{1,0:T(8,128)} %fusion.12), channel_id=1, source_target_pairs={{0,1},{1,0},{2,3},{3,2},{4,5},{5,4},{6,7},{7,6},{8,9},{9,8},{10,11... | collective-permute-start | bytes 9437192 | tf_op jit(solution)/shard_map/ppermute | solution.py:24
  66.6 36.8 %collective-permute-start.18 = (f32[512,256]{1,0:T(8,128)S(1)}, f32[512,256]{1,0:T(8,128)}, u32[]{:S(2)}, u32[]{:S(2)}) collective-permute-start(f32[512,256]{1,0:T(8,128)S(1)} %multiply_subtract_fusion.5), channel_id=1, source_target_pairs={{0,10},{2,8},{4,14},{6,12},{8,2},{10,0},{12,6},{14,4},{1,11},{3,9}... | collective-permute-start | bytes 1572872 | tf_op jit(solution)/shard_map/cond/branch_5_fun/ppermute | solution.py:17
  104.5 0.8 copy-start.3
  109.6 1.0 copy-start.4
  117.1 19.7 %collective-permute-start.22 = (f32[3072,256]{1,0:T(8,128)}, f32[3072,256]{1,0:T(8,128)}, u32[]{:S(2)}, u32[]{:S(2)}) collective-permute-start(f32[3072,256]{1,0:T(8,128)} %fusion.10), channel_id=1, source_target_pairs={{0,1},{1,0},{2,3},{3,2},{4,5},{5,4},{6,7},{7,6},{8,9},{9,8},{10,11... | collective-permute-start | bytes 9437192 | tf_op jit(solution)/shard_map/ppermute | solution.py:24
  120.6 15.4 %collective-permute-start.9 = (f32[512,256]{1,0:T(8,128)}, f32[512,256]{1,0:T(8,128)S(1)}, u32[]{:S(2)}, u32[]{:S(2)}) collective-permute-start(f32[512,256]{1,0:T(8,128)} %param.21), channel_id=1, source_target_pairs={{0,6},{2,4},{4,2},{6,0},{8,14},{10,12},{12,10},{14,8},{1,7},{3,5},... | collective-permute-start | bytes 1572872 | tf_op jit(solution)/shard_map/cond/branch_3_fun/ppermute | solution.py:17
where the time goes:
time: 143 us; the launch traced here: 142 us
  waiting for transfers between devices  51.4 us (36%)
  local copies, waits for them, and re-layouts  30.7 us (21%)
  matrix products  21.1 us (15%)
  starting transfers between devices  18 us (13%)
  other arithmetic  17.3 us (12%)
  between operations  3.24 us (2%)
    ppermute x3, waiting for transfers between devices, branch(): return lambda held: lax.ppermute(held, 'user', pairs)  51.4 us
    ppermute x3, starting transfers between devices, branch(): return lambda held: lax.ppermute(held, 'user', pairs)  18 us
    convert_element_type x2, local copies, waits for them, and re-layouts, local_grads(): dense.astype(jnp.float32)  11.1 us
    sub x2, other arithmetic, local(): user_rows - LEARNING_RATE * (grad_total + WEIGHT_DECAY * user_rows)  9.49 us
    dot_general x2, matrix products, local_grads(): lax.dot_general(user_bf, panel_bf, (((1,), (1,)), ((), ())), preferred_el...  8.99 us
    gather x2, local copies, waits for them, and re-layouts, local_grads(): jnp.take(blocks, slot_of, axis=0)  6.99 us
    dot_general x2, matrix products, local_grads(): lax.dot_general(errors, user_bf, (((0,), (0,)), ((), ())), preferred_elem...  6.76 us
    select_n x4, other arithmetic, local_grads(): jnp.take(blocks, slot_of, axis=0)  6.15 us
  transfers between devices with their start and end apart: 5, of which 3 were waited for; matrix products, arithmetic and copies ran while one was open for 14% of the time, Pallas kernels for 0%

commit v1 on v0

v1 whole, which is shorter than its diff:
```python
import functools

import jax
import jax.numpy as jnp
from jax import lax
from jax.experimental import pallas as pl
from jax.experimental.pallas import tpu as pltpu
from jax.sharding import PartitionSpec as P

LEARNING_RATE = 0.02
WEIGHT_DECAY = 0.1
TILES_PER_STEP = 2


def moved(value, partner_mask):
    count = lax.axis_size("user")

    def branch(mask):
        if mask == 0:
            return lambda held: held
        pairs = [(source, source ^ mask) for source in range(count)]
        return lambda held: lax.ppermute(held, "user", pairs)

    return lax.switch(partner_mask, [branch(mask) for mask in range(count)], value)


def item_sum(value):
    if lax.axis_size("item") == 2:
        return value + lax.ppermute(value, "item", [(0, 1), (1, 0)])
    return lax.psum(value, "item")


def grads_kernel(item_tiles, slot_ref, live_ref, user_ref, panel_ref, *rest):
    block_refs = rest[: TILES_PER_STEP * item_tiles]
    grad_user_ref, grad_panel_ref = rest[TILES_PER_STEP * item_tiles :]
    step = pl.program_id(0)
    tile_size = block_refs[0].shape[-1]

    @pl.when(step == 0)
    def _():
        grad_panel_ref[...] = jnp.zeros_like(grad_panel_ref)

    for inner in range(TILES_PER_STEP):
        rows = pl.ds(inner * tile_size, tile_size)
        user_bf = user_ref[rows, :].astype(jnp.bfloat16)
        grad_user = None
        for column in range(item_tiles):
            code = (step * TILES_PER_STEP + inner) * item_tiles + column
            live = live_ref[code].astype(jnp.float32)
            panel_bf = panel_ref[pl.ds(column * tile_size, tile_size), :]
            scores = lax.dot_general(
                user_bf, panel_bf, (((1,), (1,)), ((), ())), preferred_element_type=jnp.float32
            )
            block = block_refs[inner * item_tiles + column][...].astype(jnp.float32)
            errors = ((scores - block) * live).astype(jnp.bfloat16)
            part = lax.dot_general(
                errors, panel_bf, (((1,), (0,)), ((), ())), preferred_element_type=jnp.float32
            )
            grad_user = part if grad_user is None else grad_user + part
            cols = pl.ds(column * tile_size, tile_size)
            grad_panel_ref[cols, :] += lax.dot_general(
                errors, user_bf, (((0,), (0,)), ((), ())), preferred_element_type=jnp.float32
            )
        grad_user_ref[rows, :] = grad_user


def local_grads(user_rows, panel_bf, codes, count, blocks, first):
    tile_size = blocks.shape[-1]
    rank = user_rows.shape[1]
    user_tiles = user_rows.shape[0] // tile_size
    item_tiles = panel_bf.shape[0] // tile_size
    code_count = user_tiles * item_tiles
    slot_count = codes.shape[0]
    hits = (codes[:, None] == lax.iota(jnp.int32, code_count)[None, :]) & (
        lax.iota(jnp.int32, slot_count) < count
    )[:, None]
    live = jnp.any(hits, axis=0).astype(jnp.int32)
    slot_of = first + jnp.sum(jnp.where(hits, lax.iota(jnp.int32, slot_count)[:, None], 0), axis=0)

    def block_spec(inner, column):
        def index(step, slot_ref, live_ref):
            return (slot_ref[(step * TILES_PER_STEP + inner) * item_tiles + column], 0, 0)

        return pl.BlockSpec((None, tile_size, tile_size), index)

    rows = TILES_PER_STEP * tile_size
    grid_spec = pltpu.PrefetchScalarGridSpec(
        num_scalar_prefetch=2,
        grid=(user_tiles // TILES_PER_STEP,),
        in_specs=[
            pl.BlockSpec((rows, rank), lambda step, slot_ref, live_ref: (step, 0)),
            pl.BlockSpec((item_tiles * tile_size, rank), lambda step, slot_ref, live_ref: (0, 0)),
        ]
        + [block_spec(inner, column) for inner in range(TILES_PER_STEP) for column in range(item_tiles)],
        out_specs=[
            pl.BlockSpec((rows, rank), lambda step, slot_ref, live_ref: (step, 0)),
            pl.BlockSpec((item_tiles * tile_size, rank), lambda step, slot_ref, live_ref: (0, 0)),
        ],
    )
    flops = 3 * 2 * code_count * tile_size * tile_size * rank
    moved_bytes = user_rows.size * 4 * 2 + panel_bf.size * 2 + code_count * tile_size * tile_size * 2 + panel_bf.size * 4
    return pl.pallas_call(
        functools.partial(grads_kernel, item_tiles),
        grid_spec=grid_spec,
        out_shape=[
            jax.ShapeDtypeStruct(user_rows.shape, jnp.float32),
            jax.ShapeDtypeStruct(panel_bf.shape, jnp.float32),
        ],
        compiler_params=pltpu.CompilerParams(dimension_semantics=("arbitrary",)),
        cost_estimate=pl.CostEstimate(flops=flops, bytes_accessed=moved_bytes, transcendentals=0),
    )(slot_of, live, user_rows, panel_bf, *([blocks] * (TILES_PER_STEP * item_tiles)))


def local(user_factors, item_factors, stratum_masks, block_codes, block_counts, ratings):
    stratum_total = stratum_masks.shape[0]
    slot_count = block_codes.shape[-1] // stratum_total
    tile_size = ratings.shape[-1]
    all_blocks = ratings.reshape(-1, tile_size, tile_size)

    user_rows = user_factors
    panel_now = moved(item_factors, stratum_masks[0])
    for stratum in range(stratum_total):
        codes = block_codes[0, 0, stratum * slot_count : (stratum + 1) * slot_count]
        count = block_counts[0, 0, stratum]
        grad_user, grad_panel = local_grads(
            user_rows, panel_now.astype(jnp.bfloat16), codes, count, all_blocks, stratum * slot_count
        )
        panel_next = panel_now - LEARNING_RATE * (grad_panel + WEIGHT_DECAY * panel_now)
        if stratum + 1 < stratum_total:
            step_mask = jnp.bitwise_xor(stratum_masks[stratum], stratum_masks[stratum + 1])
        else:
            step_mask = stratum_masks[stratum]
        panel_now = moved(panel_next, step_mask)
        grad_total = item_sum(grad_user)
        user_rows = user_rows - LEARNING_RATE * (grad_total + WEIGHT_DECAY * user_rows)
    return (user_rows, panel_now)


def solution(mesh):
    placed = (
        P(("groups", "user"), None),
        P(("groups", "user", "item"), None),
        P("groups"),
        P(("groups", "user"), "item", None),
        P(("groups", "user"), "item", None),
        P(("groups", "user"), "item", None, None, None),
    )
    return jax.shard_map(
        local,
        mesh=mesh,
        in_specs=placed,
        out_specs=(P(("groups", "user"), None), P(("groups", "user", "item"), None)),
        check_vma=False,
    )
```

time: 143 us -> 146 us (1.021)
  Pallas kernels: 0 us -> 47.5 us
  local copies, waits for them, and re-layouts: 30.7 us -> 6.48 us
  matrix products: 21.1 us -> 0 us
  starting transfers between devices: 18 us -> 6.38 us
  waiting for transfers between devices: 51.4 us -> 63 us
    pallas_call x0 -> x2, Pallas kernels: none -> 47.5 us  [local_grads(): pl.pallas_call(functools.partial(grads_kernel, item_tiles), grid_spec=gri...]
    dot_general x6 -> x0, matrix products: 21.1 us -> none  [the longest x2 8.99 us: local_grads(): lax.dot_general(user_bf, panel_bf, (((1,), (1,)), ((), ())), preferred_el...]
    ppermute x3, starting transfers between devices: 18 us -> 6.3 us  [branch(): return lambda held: lax.ppermute(held, 'user', pairs)]
    ppermute x3, waiting for transfers between devices: 51.4 us -> 63 us  [branch(): return lambda held: lax.ppermute(held, 'user', pairs)]
    convert_element_type x5 -> x0, local copies, waits for them, and re-layouts: 11.4 us -> none  [the longest x2 11.1 us: local_grads(): dense.astype(jnp.float32)]
    gather x2 -> x0, local copies, waits for them, and re-layouts: 6.99 us -> none  [local_grads(): jnp.take(blocks, slot_of, axis=0)]
    select_n x4 -> x0, other arithmetic: 6.15 us -> none  [local_grads(): jnp.take(blocks, slot_of, axis=0)]
    squeeze x1 -> x0, local copies, waits for them, and re-layouts: 4.01 us -> none  [local(): blocks = ratings[0, 0, stratum * slot_count:(stratum + 1) * slot_count]]
  transfers between devices with their start and end apart: 5 -> 5, of which waited for: 3 -> 3; matrix products, arithmetic and copies ran while one was open for 14% -> 5% of each run, Pallas kernels for 0% -> 0%
where the time goes in v1:
time: 146 us; the launch traced here: 145 us
  waiting for transfers between devices  63 us (43%)
  Pallas kernels  47.5 us (33%)
  other arithmetic  18.6 us (13%)
  local copies, waits for them, and re-layouts  6.48 us (4%)
  starting transfers between devices  6.38 us (4%)
  between operations  3.15 us (2%)
    ppermute x3, waiting for transfers between devices, branch(): return lambda held: lax.ppermute(held, 'user', pairs)  63 us
    pallas_call x2, Pallas kernels, local_grads(): pl.pallas_call(functools.partial(grads_kernel, item_tiles), grid_spec=gri...  47.5 us
    sub x2, other arithmetic, local(): user_rows - LEARNING_RATE * (grad_total + WEIGHT_DECAY * user_rows)  11.2 us
    ppermute x3, starting transfers between devices, branch(): return lambda held: lax.ppermute(held, 'user', pairs)  6.3 us
  transfers between devices with their start and end apart: 5, of which 3 were waited for; matrix products, arithmetic and copies ran while one was open for 5% of the time, Pallas kernels for 0%

profile of v1, /device:TPU:0, one launch (start us, length us, event | category | flops | bytes accessed | tf_op | source)
XLA Modules:
  0.0 145.2 jit_solution(795124110881552171)
XLA Ops:
  0.6 1.0 copy.57
  1.7 0.8 slice_bitcast_fusion
  2.5 1.4 fusion.5
  3.9 0.6 iota_compare_fusion.3
  4.5 0.1 fusion.1
  4.6 0.6 select_reduce_fusion.1.slot_ref
  5.2 1.3 fusion.4
  6.6 0.5 convert_element_type.12.live_ref
  7.8 27.3 %conditional.5 = (f32[512,256]{1,0:T(8,128)S(1)}) conditional(s32[]{:T(128)} %bitcast.2, f32[512,256]{1,0:T(8,128)S(1)} %copy.57, f32[512,256]{1,0:T(8,128)S(1)} %copy.57, f32[512,256]{1,0:T(8,128)S(1)} %copy.57, f32[512,256]{1,0:T(8,128)S(1)} %copy.57, f32[512,256]{1,0:T(8,128)S(1)} %copy.57, ...), branch_computations={%region_2.0_spmd, %region_3.0_spmd, %region_4.0_spmd, %region_5.0_... | conditional | bytes 3145776 | solution.py:24
  7.8 4.1 %collective-permute-start.3 = (f32[512,256]{1,0:T(8,128)S(1)}, f32[512,256]{1,0:T(8,128)S(1)}, u32[]{:S(2)}, u32[]{:S(2)}) collective-permute-start(f32[512,256]{1,0:T(8,128)S(1)} %param.4), channel_id=1, source_target_pairs={{0,8},{2,10},{4,12},{6,14},{8,0},{10,2},{12,4},{14,6},{1,9},{3,11}... | collective-permute-start | bytes 1572872 | tf_op jit(solution)/shard_map/cond/branch_4_fun/ppermute | solution.py:22
  11.9 23.2 %collective-permute-done.3 = f32[512,256]{1,0:T(8,128)S(1)} collective-permute-done((f32[512,256]{1,0:T(8,128)S(1)}, f32[512,256]{1,0:T(8,128)S(1)}, u32[]{:S(2)}, u32[]{:S(2)}) %collective-permute-start.3) | collective-permute-done | bytes 524320 | tf_op jit(solution)/shard_map/cond/branch_4_fun/ppermute | solution.py:22
  35.1 0.7 convert_element_type.13.panel_ref
  35.8 23.6 %shard_map.101 = (f32[3072,256]{1,0:T(8,128)}, f32[512,256]{1,0:T(8,128)S(1)}) custom-call(s32[96]{0:T(128)} %select_reduce_fusion.1.slot_ref, s32[96]{0:T(128)} %convert_element_type.12.live_ref, f32[3072,256]{1,0:T(8,128)} %user_ref.1, bf16[512,256]{1,0:T(8,128)(2,1)} %convert_element_type.13.panel_ref, bf16[128,128,128]{2,1,0:T(8,128)(2,1)} %bitcast.10, ...), custom_call_target="tpu_custom_call" | custom-call | flops 2415919104 | bytes 10223616 | tf_op jit(solution)/shard_map/pallas_call | solution.py:102
  60.7 0.6 iota_compare_fusion.2
  61.4 0.1 fusion.3
  61.5 0.5 convert_element_type.14.live_ref
  62.0 28.7 %conditional.8 = (f32[512,256]{1,0:T(8,128)}, f32[512,256]{1,0:T(8,128)S(1)}) conditional(s32[]{:T(128)} %bitcast.6, (f32[512,256]{1,0:T(8,128)S(1)}, f32[512,256]{1,0:T(8,128)S(1)}, f32[512,256]{1,0:T(8,128)S(1)}) %tuple.164, (f32[512,256]{1,0:T(8,128)S(1)}, f32[512,256]{1,0:T(8,128)S(1)}, ...), branch_computations={%region_12.13_spmd, %region_13.14_spmd, %region_14.15_spmd, %regio... | conditional | flops 524288 | bytes 5242936
  62.0 0.1 multiply_subtract_fusion.5
  62.2 0.6 collective-permute-start.18
  62.7 27.0 %collective-permute-done.18 = f32[512,256]{1,0:T(8,128)} collective-permute-done((f32[512,256]{1,0:T(8,128)S(1)}, f32[512,256]{1,0:T(8,128)}, u32[]{:S(2)}, u32[]{:S(2)}) %collective-permute-start.18) | collective-permute-done | bytes 524320 | tf_op jit(solution)/shard_map/cond/branch_5_fun/ppermute | solution.py:22
  89.7 1.0 copy.54
  90.7 0.7 convert_element_type.24.panel_ref
  91.5 0.1 select_reduce_fusion
  91.5 0.5 broadcast_add_fusion.slot_ref
  92.1 6.0 %multiply_subtract_fusion.9.user_ref = f32[3072,256]{1,0:T(8,128)} fusion(f32[3072,256]{1,0:T(8,128)} %user_ref.1, f32[3072,256]{1,0:T(8,128)} %get-tuple-element.186, f32[3072,256]{1,0:T(8,128)} %collective-permute-done.21), kind=kLoop, calls=%fused_computation.9 | loop fusion | flops 3932160 | bytes 12582912 | tf_op jit(solution)/shard_map/sub | solution.py:135
  98.1 23.9 %shard_map.102 = (f32[3072,256]{1,0:T(8,128)}, f32[512,256]{1,0:T(8,128)}) custom-call(s32[96]{0:T(128)} %broadcast_add_fusion.slot_ref, s32[96]{0:T(128)} %convert_element_type.14.live_ref, f32[3072,256]{1,0:T(8,128)} %multiply_subtract_fusion.9.user_ref, bf16[512,256]{1,0:T(8,128)(2,1)} %convert_element_type.24.panel_ref, bf16[128,128,128]{2,1,0:T(8,128)(2,1)} %bitcast.18, ...), custom_call_target="tpu_custom_call" | custom-call | flops 2415919104 | bytes 10223616 | tf_op jit(solution)/shard_map/pallas_call | solution.py:102
  122.7 2.1 %multiply_subtract_fusion.10 = f32[512,256]{1,0:T(8,128)} fusion(f32[512,256]{1,0:T(8,128)} %get-tuple-element.190, f32[512,256]{1,0:T(8,128)} %get-tuple-element.191), kind=kLoop, calls=%fused_computation.10 | loop fusion | flops 524288 | bytes 1572864 | tf_op jit(solution)/shard_map/sub | solution.py:128
  124.8 15.3 %conditional.7 = (f32[512,256]{1,0:T(8,128)}) conditional(s32[]{:T(128)} %bitcast.7, f32[512,256]{1,0:T(8,128)} %multiply_subtract_fusion.10, f32[512,256]{1,0:T(8,128)} %multiply_subtract_fusion.10, f32[512,256]{1,0:T(8,128)} %multiply_subtract_fusion.10, f32[512,256]{1,0:T(8,128)} %multiply_subtract_fusion.10, ...), branch_computations={%region_20.21_spmd, %region_21.22_spmd, %region_22.23_spmd, %regio... | conditional | bytes 3145776 | solution.py:24
  124.8 1.6 %collective-permute-start.7 = (f32[512,256]{1,0:T(8,128)}, f32[512,256]{1,0:T(8,128)S(1)}, u32[]{:S(2)}, u32[]{:S(2)}) collective-permute-start(f32[512,256]{1,0:T(8,128)} %param.17), channel_id=1, source_target_pairs={{0,2},{2,0},{4,6},{6,4},{8,10},{10,8},{12,14},{14,12},{1,3},{3,1},... | collective-permute-start | bytes 1572872 | tf_op jit(solution)/shard_map/cond/branch_1_fun/ppermute | solution.py:22
  126.4 12.9 %collective-permute-done.7 = f32[512,256]{1,0:T(8,128)S(1)} collective-permute-done((f32[512,256]{1,0:T(8,128)}, f32[512,256]{1,0:T(8,128)S(1)}, u32[]{:S(2)}, u32[]{:S(2)}) %collective-permute-start.7) | collective-permute-done | bytes 524320 | tf_op jit(solution)/shard_map/cond/branch_1_fun/ppermute | solution.py:22
  139.3 0.8 copy.33
  140.1 5.1 %multiply_subtract_fusion.8 = f32[3072,256]{1,0:T(8,128)} fusion(f32[3072,256]{1,0:T(8,128)S(1)} %copy-done, f32[3072,256]{1,0:T(8,128)} %get-tuple-element.189, f32[3072,256]{1,0:T(8,128)} %collective-permute-done.22), kind=kLoop, calls=%fused_computation.8 | loop fusion | flops 3932160 | bytes 12582912 | tf_op jit(solution)/shard_map/sub | solution.py:135
  (8 shorter events, 0.2 us)
Async XLA Ops:
  7.8 27.3 %collective-permute-start.3 = (f32[512,256]{1,0:T(8,128)S(1)}, f32[512,256]{1,0:T(8,128)S(1)}, u32[]{:S(2)}, u32[]{:S(2)}) collective-permute-start(f32[512,256]{1,0:T(8,128)S(1)} %param.4), channel_id=1, source_target_pairs={{0,8},{2,10},{4,12},{6,14},{8,0},{10,2},{12,4},{14,6},{1,9},{3,11}... | collective-permute-start | bytes 1572872 | tf_op jit(solution)/shard_map/cond/branch_4_fun/ppermute | solution.py:22
  59.5 32.6 %collective-permute-start.21 = (f32[3072,256]{1,0:T(8,128)}, f32[3072,256]{1,0:T(8,128)}, u32[]{:S(2)}, u32[]{:S(2)}) collective-permute-start(f32[3072,256]{1,0:T(8,128)} %get-tuple-element.186), channel_id=1, source_target_pairs={{0,1},{1,0},{2,3},{3,2},{4,5},{5,4},{6,7},{7,6},{8,9},{9,8},{10,11... | collective-permute-start | bytes 9437192 | tf_op jit(solution)/shard_map/ppermute | solution.py:29
  62.2 27.5 %collective-permute-start.18 = (f32[512,256]{1,0:T(8,128)S(1)}, f32[512,256]{1,0:T(8,128)}, u32[]{:S(2)}, u32[]{:S(2)}) collective-permute-start(f32[512,256]{1,0:T(8,128)S(1)} %multiply_subtract_fusion.5), channel_id=1, source_target_pairs={{0,10},{2,8},{4,14},{6,12},{8,2},{10,0},{12,6},{14,4},{1,11},{3,9}... | collective-permute-start | bytes 1572872 | tf_op jit(solution)/shard_map/cond/branch_5_fun/ppermute | solution.py:22
  122.0 18.1 %collective-permute-start.22 = (f32[3072,256]{1,0:T(8,128)}, f32[3072,256]{1,0:T(8,128)}, u32[]{:S(2)}, u32[]{:S(2)}) collective-permute-start(f32[3072,256]{1,0:T(8,128)} %get-tuple-element.189), channel_id=1, source_target_pairs={{0,1},{1,0},{2,3},{3,2},{4,5},{5,4},{6,7},{7,6},{8,9},{9,8},{10,11... | collective-permute-start | bytes 9437192 | tf_op jit(solution)/shard_map/ppermute | solution.py:29
  124.8 15.3 %copy-start = (f32[3072,256]{1,0:T(8,128)S(1)}, f32[3072,256]{1,0:T(8,128)}, u32[]{:S(2)}) copy-start(f32[3072,256]{1,0:T(8,128)} %multiply_subtract_fusion.9.user_ref) | copy-start | bytes 9437188
  124.8 14.5 %collective-permute-start.7 = (f32[512,256]{1,0:T(8,128)}, f32[512,256]{1,0:T(8,128)S(1)}, u32[]{:S(2)}, u32[]{:S(2)}) collective-permute-start(f32[512,256]{1,0:T(8,128)} %param.17), channel_id=1, source_target_pairs={{0,2},{2,0},{4,6},{6,4},{8,10},{10,8},{12,14},{14,12},{1,3},{3,1},... | collective-permute-start | bytes 1572872 | tf_op jit(solution)/shard_map/cond/branch_1_fun/ppermute | solution.py:22

commit v2 on v1

v2 whole, which is shorter than its diff:
```python
import functools

import jax
import jax.numpy as jnp
from jax import lax
from jax.experimental import pallas as pl
from jax.experimental.pallas import tpu as pltpu
from jax.sharding import PartitionSpec as P

LEARNING_RATE = 0.02
WEIGHT_DECAY = 0.1
TILES_PER_STEP = 4


def moved(value, partner_mask):
    count = lax.axis_size("user")

    def branch(mask):
        if mask == 0:
            return lambda held: held
        pairs = [(source, source ^ mask) for source in range(count)]
        return lambda held: lax.ppermute(held, "user", pairs)

    return lax.switch(partner_mask, [branch(mask) for mask in range(count)], value)


def item_sum(value):
    if lax.axis_size("item") == 2:
        return value + lax.ppermute(value, "item", [(0, 1), (1, 0)])
    return lax.psum(value, "item")


def grads_kernel(item_tiles, slot_ref, live_ref, user_ref, user_t_ref, panel_ref, panel_t_ref, *rest):
    block_refs = rest[: TILES_PER_STEP * item_tiles]
    grad_user_ref, grad_panel_t_ref = rest[TILES_PER_STEP * item_tiles :]
    step = pl.program_id(0)
    tile_size = block_refs[0].shape[-1]

    @pl.when(step == 0)
    def _():
        grad_panel_t_ref[...] = jnp.zeros_like(grad_panel_t_ref)

    scores = jnp.dot(user_ref[...], panel_t_ref[...], preferred_element_type=jnp.float32)
    pieces = []
    for inner in range(TILES_PER_STEP):
        row = []
        for column in range(item_tiles):
            code = (step * TILES_PER_STEP + inner) * item_tiles + column
            live = live_ref[code].astype(jnp.float32)
            block = block_refs[inner * item_tiles + column][...].astype(jnp.float32)
            part = scores[inner * tile_size : (inner + 1) * tile_size, column * tile_size : (column + 1) * tile_size]
            row.append(((part - block) * live).astype(jnp.bfloat16))
        pieces.append(jnp.concatenate(row, axis=1))
    errors = jnp.concatenate(pieces, axis=0)
    grad_user_ref[...] = jnp.dot(errors, panel_ref[...], preferred_element_type=jnp.float32)
    grad_panel_t_ref[...] += jnp.dot(user_t_ref[...], errors, preferred_element_type=jnp.float32)


def local_grads(user_bf, user_t, panel_bf, panel_t, codes, count, blocks, first):
    tile_size = blocks.shape[-1]
    rank = user_bf.shape[1]
    user_tiles = user_bf.shape[0] // tile_size
    item_tiles = panel_bf.shape[0] // tile_size
    code_count = user_tiles * item_tiles
    slot_count = codes.shape[0]
    hits = (codes[:, None] == lax.iota(jnp.int32, code_count)[None, :]) & (
        lax.iota(jnp.int32, slot_count) < count
    )[:, None]
    live = jnp.any(hits, axis=0).astype(jnp.int32)
    slot_of = first + jnp.sum(jnp.where(hits, lax.iota(jnp.int32, slot_count)[:, None], 0), axis=0)

    def block_spec(inner, column):
        def index(step, slot_ref, live_ref):
            return (slot_ref[(step * TILES_PER_STEP + inner) * item_tiles + column], 0, 0)

        return pl.BlockSpec((None, tile_size, tile_size), index)

    rows = TILES_PER_STEP * tile_size
    columns = item_tiles * tile_size
    grid_spec = pltpu.PrefetchScalarGridSpec(
        num_scalar_prefetch=2,
        grid=(user_tiles // TILES_PER_STEP,),
        in_specs=[
            pl.BlockSpec((rows, rank), lambda step, slot_ref, live_ref: (step, 0)),
            pl.BlockSpec((rank, rows), lambda step, slot_ref, live_ref: (0, step)),
            pl.BlockSpec((columns, rank), lambda step, slot_ref, live_ref: (0, 0)),
            pl.BlockSpec((rank, columns), lambda step, slot_ref, live_ref: (0, 0)),
        ]
        + [block_spec(inner, column) for inner in range(TILES_PER_STEP) for column in range(item_tiles)],
        out_specs=[
            pl.BlockSpec((rows, rank), lambda step, slot_ref, live_ref: (step, 0)),
            pl.BlockSpec((rank, columns), lambda step, slot_ref, live_ref: (0, 0)),
        ],
    )
    flops = 3 * 2 * code_count * tile_size * tile_size * rank
    moved_bytes = user_bf.size * 2 * 2 + user_bf.size * 4 + panel_bf.size * 8 + code_count * tile_size * tile_size * 2
    return pl.pallas_call(
        functools.partial(grads_kernel, item_tiles),
        grid_spec=grid_spec,
        out_shape=[
            jax.ShapeDtypeStruct(user_bf.shape, jnp.float32),
            jax.ShapeDtypeStruct(panel_t.shape, jnp.float32),
        ],
        compiler_params=pltpu.CompilerParams(dimension_semantics=("arbitrary",)),
        cost_estimate=pl.CostEstimate(flops=flops, bytes_accessed=moved_bytes, transcendentals=0),
    )(slot_of, live, user_bf, user_t, panel_bf, panel_t, *([blocks] * (TILES_PER_STEP * item_tiles)))


def local(user_factors, item_factors, stratum_masks, block_codes, block_counts, ratings):
    stratum_total = stratum_masks.shape[0]
    slot_count = block_codes.shape[-1] // stratum_total
    tile_size = ratings.shape[-1]
    all_blocks = ratings.reshape(-1, tile_size, tile_size)

    user_rows = user_factors
    panel_now = moved(item_factors, stratum_masks[0])
    for stratum in range(stratum_total):
        codes = block_codes[0, 0, stratum * slot_count : (stratum + 1) * slot_count]
        count = block_counts[0, 0, stratum]
        user_bf = user_rows.astype(jnp.bfloat16)
        panel_bf = panel_now.astype(jnp.bfloat16)
        grad_user, grad_panel_t = local_grads(
            user_bf, user_bf.T, panel_bf, panel_bf.T, codes, count, all_blocks, stratum * slot_count
        )
        panel_next = panel_now - LEARNING_RATE * (grad_panel_t.T + WEIGHT_DECAY * panel_now)
        if stratum + 1 < stratum_total:
            step_mask = jnp.bitwise_xor(stratum_masks[stratum], stratum_masks[stratum + 1])
        else:
            step_mask = stratum_masks[stratum]
        panel_now = moved(panel_next, step_mask)
        grad_total = item_sum(grad_user)
        user_rows = user_rows - LEARNING_RATE * (grad_total + WEIGHT_DECAY * user_rows)
    return (user_rows, panel_now)


def solution(mesh):
    placed = (
        P(("groups", "user"), None),
        P(("groups", "user", "item"), None),
        P("groups"),
        P(("groups", "user"), "item", None),
        P(("groups", "user"), "item", None),
        P(("groups", "user"), "item", None, None, None),
    )
    return jax.shard_map(
        local,
        mesh=mesh,
        in_specs=placed,
        out_specs=(P(("groups", "user"), None), P(("groups", "user", "item"), None)),
        check_vma=False,
    )
```

time: 146 us -> 152 us (1.041)
  the two profiles are of different devices: /device:TPU:0 before, /device:TPU:18 now
where the time goes in v2:
time: 152 us; the launch traced here: 151 us
  waiting for transfers between devices  62.2 us (41%)
  local copies, waits for them, and re-layouts  38.2 us (25%)
  other arithmetic  23.5 us (15%)
  Pallas kernels  17.9 us (12%)
  starting transfers between devices  5.68 us (4%)
  between operations  3.22 us (2%)
    ppermute x3, waiting for transfers between devices, branch(): return lambda held: lax.ppermute(held, 'user', pairs)  62.2 us
    pallas_call x2, Pallas kernels, local_grads(): pl.pallas_call(functools.partial(grads_kernel, item_tiles), grid_spec=gri...  17.9 us
    unnamed x9, local copies, waits for them, and re-layouts  10.5 us
    sub x1, other arithmetic, local(): user_rows - LEARNING_RATE * (grad_total + WEIGHT_DECAY * user_rows)  8.35 us
    another operation x6, local copies, waits for them, and re-layouts  7.79 us
    pallas_call x2, local copies, waits for them, and re-layouts, local_grads(): pl.pallas_call(functools.partial(grads_kernel, item_tiles), grid_spec=gri...  7.09 us
    convert_element_type x2, other arithmetic, local(): user_bf = user_rows.astype(jnp.bfloat16)  6.39 us
    ppermute x3, starting transfers between devices, branch(): return lambda held: lax.ppermute(held, 'user', pairs)  5.66 us
  transfers between devices with their start and end apart: 5, of which 3 were waited for; matrix products, arithmetic and copies ran while one was open for 10% of the time, Pallas kernels for 0%

profile of v2, /device:TPU:18, one launch (start us, length us, event | category | flops | bytes accessed | tf_op | source)
XLA Modules:
  0.0 150.7 jit_solution(7021761075161078882)
XLA Ops:
  0.6 1.9 %copy.128 = f32[512,256]{1,0:T(8,128)} copy(f32[512,256]{1,0:T(8,128)} %param.31) | data formatting | bytes 1048576
  3.3 1.3 fusion.9
  6.0 2.4 %copy.54 = f32[3072,256]{0,1:T(8,128)S(1)} copy(f32[3072,256]{1,0:T(8,128)} %param.30) | data formatting | bytes 6291456 | tf_op args[0]
  8.4 1.4 convert_bitcast_fusion.user_t_ref
  9.8 1.4 convert_element_type.19
  13.0 23.9 %conditional.5 = (f32[512,256]{1,0:T(8,128)}) conditional(s32[]{:T(128)} %bitcast.3, f32[512,256]{1,0:T(8,128)} %copy.128, f32[512,256]{1,0:T(8,128)} %copy.128, f32[512,256]{1,0:T(8,128)} %copy.128, f32[512,256]{1,0:T(8,128)} %copy.128, f32[512,256]{1,0:T(8,128)} %copy.128, f32[512,256]{1,0:T(8,128)} %copy.128, ...), branch_computations={%region_2.0_spmd, %region_3.0_spmd, %region_4.0_spmd, %region_5.0_... | conditional | bytes 3145776 | solution.py:24
  13.1 23.0 %collective-permute-done.4 = f32[512,256]{1,0:T(8,128)S(1)} collective-permute-done((f32[512,256]{1,0:T(8,128)}, f32[512,256]{1,0:T(8,128)S(1)}, u32[]{:S(2)}, u32[]{:S(2)}) %collective-permute-start.4) | collective-permute-done | bytes 524320 | tf_op jit(solution)/shard_map/cond/branch_5_fun/ppermute | solution.py:22
  36.9 1.2 copy.48
  38.1 0.8 copy.50.panel_ref
  38.9 2.6 %copy.49.user_ref = bf16[3072,256]{1,0:T(8,128)(2,1)} copy(bf16[3072,256]{0,1:T(8,128)(2,1)} %convert_element_type.19) | data formatting | bytes 3145728 | tf_op jit(solution)/shard_map/convert_element_type | solution.py:120
  41.5 9.0 %shard_map.101 = (f32[3072,256]{1,0:T(8,128)}, f32[256,512]{1,0:T(8,128)}) custom-call(s32[96]{0:T(128)} %select_reduce_fusion.1.slot_ref, s32[96]{0:T(128)} %convert_element_type.18.live_ref, bf16[3072,256]{1,0:T(8,128)(2,1)} %copy.49.user_ref, bf16[256,3072]{1,0:T(8,128)(2,1)} %convert_bitcast_fusion.user_t_ref, bf16[512,256]{1,0:T(8,128)(2,1)} %copy.50.panel_ref, ...), custom_call_target="tpu_custom_call" | custom-call | flops 2415919104 | bytes 10485760 | tf_op jit(solution)/shard_map/pallas_call | solution.py:97
  50.4 3.5 %copy.52 = f32[3072,256]{0,1:T(8,128)} copy(f32[3072,256]{1,0:T(8,128)} %get-tuple-element.186) | data formatting | bytes 6291456 | tf_op jit(solution)/shard_map/pallas_call | solution.py:97
  56.5 0.9 broadcast.46
  57.3 26.4 %conditional.6 = (bf16[512,256]{1,0:T(8,128)(2,1)S(1)}, f32[512,256]{0,1:T(8,128)}) conditional(s32[]{:T(128)} %bitcast.9, (f32[512,256]{1,0:T(8,128)}, f32[512,256]{0,1:T(8,128)}, f32[512,256]{0,1:T(8,128)}) %tuple.230, (f32[512,256]{1,0:T(8,128)}, f32[512,256]{0,1:T(8,128)}, f32[512,256]{0,1:T(8,128)}) %tuple.231, ...), branch_computations={%region_12.13_spmd, %region_13.14_spmd, %region_14.15_spmd, %regio... | conditional | flops 655360 | bytes 10223700
  57.3 2.0 %copy.60 = f32[512,256]{1,0:T(8,128)} copy(f32[512,256]{0,1:T(8,128)} %get-tuple-element.227) | data formatting | bytes 1048576 | tf_op jit(solution)/shard_map
  59.3 2.1 %copy.59 = f32[512,256]{1,0:T(8,128)} copy(f32[512,256]{0,1:T(8,128)} %get-tuple-element.226) | data formatting | bytes 1048576 | tf_op jit(solution)/shard_map
  61.4 1.5 multiply_subtract_fusion.2
  62.9 5.6 %collective-permute-start.15 = (f32[512,256]{1,0:T(8,128)S(1)}, f32[512,256]{1,0:T(8,128)S(1)}, u32[]{:S(2)}, u32[]{:S(2)}) collective-permute-start(f32[512,256]{1,0:T(8,128)S(1)} %multiply_subtract_fusion.2), channel_id=1, source_target_pairs={{0,4},{2,6},{4,0},{6,2},{8,12},{10,14},{12,8},{14,10},{1,5},{3,7},... | collective-permute-start | bytes 1572872 | tf_op jit(solution)/shard_map/cond/branch_2_fun/ppermute | solution.py:22
  68.5 12.4 %collective-permute-done.15 = f32[512,256]{1,0:T(8,128)S(1)} collective-permute-done((f32[512,256]{1,0:T(8,128)S(1)}, f32[512,256]{1,0:T(8,128)S(1)}, u32[]{:S(2)}, u32[]{:S(2)}) %collective-permute-start.15) | collective-permute-done | bytes 524320 | tf_op jit(solution)/shard_map/cond/branch_2_fun/ppermute | solution.py:22
  81.7 2.1 %copy.88 = f32[512,256]{0,1:T(8,128)} copy(f32[512,256]{1,0:T(8,128)} %copy-done.2) | data formatting | bytes 1048576 | tf_op jit(solution)/shard_map/conditional.1
  83.8 0.8 copy.71
  85.2 5.0 %fusion.6 = bf16[3072,256]{0,1:T(8,128)(2,1)} fusion(f32[3072,256]{0,1:T(8,128)S(1)} %copy.54, f32[3072,256]{0,1:T(8,128)} %copy.52, f32[3072,256]{0,1:T(8,128)} %collective-permute-done.21), kind=kLoop, calls=%fused_computation.26 | loop fusion | flops 4718592 | bytes 11010048 | tf_op jit(solution)/shard_map/convert_element_type | solution.py:120
  90.3 2.6 %copy.72.user_ref = bf16[3072,256]{1,0:T(8,128)(2,1)} copy(bf16[3072,256]{0,1:T(8,128)(2,1)} %fusion.6) | data formatting | bytes 3145728 | tf_op jit(solution)/shard_map/convert_element_type | solution.py:120
  92.9 8.9 %shard_map.102 = (f32[3072,256]{1,0:T(8,128)}, f32[256,512]{1,0:T(8,128)}) custom-call(s32[96]{0:T(128)} %broadcast_add_fusion.slot_ref, s32[96]{0:T(128)} %convert_element_type.21.live_ref, bf16[3072,256]{1,0:T(8,128)(2,1)} %copy.72.user_ref, bf16[256,3072]{1,0:T(8,128)(2,1)} %bitcast.62, bf16[512,256]{1,0:T(8,128)(2,1)S(1)} %get-tuple-element.192.panel_ref, ...), custom_call_target="tpu_custom_call" | custom-call | flops 2415919104 | bytes 10485760 | tf_op jit(solution)/shard_map/pallas_call | solution.py:97
  101.8 3.6 %copy.74 = f32[3072,256]{0,1:T(8,128)} copy(f32[3072,256]{1,0:T(8,128)} %get-tuple-element.189) | data formatting | bytes 6291456 | tf_op jit(solution)/shard_map/pallas_call | solution.py:97
  106.1 2.1 %fusion.1 = f32[512,256]{0,1:T(8,128)} fusion(f32[512,256]{0,1:T(8,128)} %get-tuple-element.245, f32[256,512]{1,0:T(8,128)} %get-tuple-element.191), kind=kLoop, calls=%fused_computation.12 | loop fusion | flops 524288 | bytes 1572864 | tf_op jit(solution)/shard_map/sub | solution.py:125
  108.2 28.8 %conditional.7 = (f32[512,256]{1,0:T(8,128)}) conditional(s32[]{:T(128)} %bitcast.12, f32[512,256]{0,1:T(8,128)} %fusion.1, f32[512,256]{0,1:T(8,128)} %fusion.1, f32[512,256]{0,1:T(8,128)} %fusion.1, f32[512,256]{0,1:T(8,128)} %fusion.1, f32[512,256]{0,1:T(8,128)} %fusion.1, f32[512,256]{0,1:T(8,128)} %fusion.1, ...), branch_computations={%region_20.21_spmd, %region_21.22_spmd, %region_22.23_spmd, %regio... | conditional | bytes 3145776 | solution.py:24
  108.2 2.0 %copy.84 = f32[512,256]{1,0:T(8,128)} copy(f32[512,256]{0,1:T(8,128)} %param.23) | data formatting | bytes 1048576 | tf_op jit(solution)/shard_map/sub
  110.2 26.8 %collective-permute-done.13 = f32[512,256]{1,0:T(8,128)} collective-permute-done((f32[512,256]{1,0:T(8,128)}, f32[512,256]{1,0:T(8,128)}, u32[]{:S(2)}, u32[]{:S(2)}) %collective-permute-start.13) | collective-permute-done | bytes 524320 | tf_op jit(solution)/shard_map/cond/branch_7_fun/ppermute | solution.py:22
  137.0 8.3 %multiply_subtract_fusion.8 = f32[3072,256]{0,1:T(8,128)} fusion(f32[3072,256]{0,1:T(8,128)} %copy.74, f32[3072,256]{0,1:T(8,128)} %collective-permute-done.22, f32[3072,256]{0,1:T(8,128)S(1)} %copy.54, f32[3072,256]{0,1:T(8,128)} %copy.52, f32[3072,256]{0,1:T(8,128)} %collective-permute-done.21), kind=kLoop, calls=%fused_computation.8 | loop fusion | flops 7864320 | bytes 18874368 | tf_op jit(solution)/shard_map/sub | solution.py:132
  145.3 3.5 %copy.85 = f32[3072,256]{1,0:T(8,128)} copy(f32[3072,256]{0,1:T(8,128)} %multiply_subtract_fusion.8) | data formatting | bytes 6291456
  148.9 1.9 %copy.129 = f32[512,256]{1,0:T(8,128)} copy(f32[512,256]{1,0:T(8,128)} %get-tuple-element.275) | data formatting | bytes 1048576
  (25 shorter events, 6.9 us)
Async XLA Ops:
  9.8 1.4 copy-start.8
  13.0 23.1 %collective-permute-start.4 = (f32[512,256]{1,0:T(8,128)}, f32[512,256]{1,0:T(8,128)S(1)}, u32[]{:S(2)}, u32[]{:S(2)}) collective-permute-start(f32[512,256]{1,0:T(8,128)} %param.5), channel_id=1, source_target_pairs={{0,10},{2,8},{4,14},{6,12},{8,2},{10,0},{12,6},{14,4},{1,11},{3,9}... | collective-permute-start | bytes 1572872 | tf_op jit(solution)/shard_map/cond/branch_5_fun/ppermute | solution.py:22
  38.1 3.4 %copy-start = (bf16[512,256]{0,1:T(8,128)(2,1)}, bf16[512,256]{0,1:T(8,128)(2,1)S(1)}, u32[]{:S(2)}) copy-start(bf16[512,256]{0,1:T(8,128)(2,1)S(1)} %copy.48) | copy-start | bytes 786436
  54.0 31.3 %collective-permute-start.21 = (f32[3072,256]{0,1:T(8,128)}, f32[3072,256]{0,1:T(8,128)}, u32[]{:S(2)}, u32[]{:S(2)}) collective-permute-start(f32[3072,256]{0,1:T(8,128)} %copy.52), channel_id=1, source_target_pairs={{0,1},{1,0},{2,3},{3,2},{4,5},{5,4},{6,7},{7,6},{8,9},{9,8},{10,11... | collective-permute-start | bytes 9437192 | tf_op jit(solution)/shard_map/ppermute | solution.py:29
  62.9 18.0 %collective-permute-start.15 = (f32[512,256]{1,0:T(8,128)S(1)}, f32[512,256]{1,0:T(8,128)S(1)}, u32[]{:S(2)}, u32[]{:S(2)}) collective-permute-start(f32[512,256]{1,0:T(8,128)S(1)} %multiply_subtract_fusion.2), channel_id=1, source_target_pairs={{0,4},{2,6},{4,0},{6,2},{8,12},{10,14},{12,8},{14,10},{1,5},{3,7},... | collective-permute-start | bytes 1572872 | tf_op jit(solution)/shard_map/cond/branch_2_fun/ppermute | solution.py:22
  80.9 0.8 copy-start.2
  105.4 31.6 %collective-permute-start.22 = (f32[3072,256]{0,1:T(8,128)}, f32[3072,256]{0,1:T(8,128)}, u32[]{:S(2)}, u32[]{:S(2)}) collective-permute-start(f32[3072,256]{0,1:T(8,128)} %copy.74), channel_id=1, source_target_pairs={{0,1},{1,0},{2,3},{3,2},{4,5},{5,4},{6,7},{7,6},{8,9},{9,8},{10,11... | collective-permute-start | bytes 9437192 | tf_op jit(solution)/shard_map/ppermute | solution.py:29
  110.2 26.8 %collective-permute-start.13 = (f32[512,256]{1,0:T(8,128)}, f32[512,256]{1,0:T(8,128)}, u32[]{:S(2)}, u32[]{:S(2)}) collective-permute-start(f32[512,256]{1,0:T(8,128)} %copy.84), channel_id=1, source_target_pairs={{0,14},{2,12},{4,10},{6,8},{8,6},{10,4},{12,2},{14,0},{1,15},{3,13... | collective-permute-start | bytes 1572872 | tf_op jit(solution)/shard_map/cond/branch_7_fun/ppermute | solution.py:22

commit v3 on v1

--- a/solution.py
+++ b/solution.py
@@ -9,7 +9,7 @@
 
 LEARNING_RATE = 0.02
 WEIGHT_DECAY = 0.1
-TILES_PER_STEP = 2
+TILES_PER_STEP = 4
 
 
 def moved(value, partner_mask):
@@ -40,28 +40,26 @@
     def _():
         grad_panel_ref[...] = jnp.zeros_like(grad_panel_ref)
 
+    user_bf = user_ref[...].astype(jnp.bfloat16)
+    panel_bf = panel_ref[...]
+    scores = lax.dot_general(
+        user_bf, panel_bf, (((1,), (1,)), ((), ())), preferred_element_type=jnp.float32
+    )
+    pieces = []
     for inner in range(TILES_PER_STEP):
-        rows = pl.ds(inner * tile_size, tile_size)
-        user_bf = user_ref[rows, :].astype(jnp.bfloat16)
-        grad_user = None
+        row = []
         for column in range(item_tiles):
             code = (step * TILES_PER_STEP + inner) * item_tiles + column
             live = live_ref[code].astype(jnp.float32)
-            panel_bf = panel_ref[pl.ds(column * tile_size, tile_size), :]
-            scores = lax.dot_general(
-                user_bf, panel_bf, (((1,), (1,)), ((), ())), preferred_element_type=jnp.float32
-            )
             block = block_refs[inner * item_tiles + column][...].astype(jnp.float32)
-            errors = ((scores - block) * live).astype(jnp.bfloat16)
-            part = lax.dot_general(
-                errors, panel_bf, (((1,), (0,)), ((), ())), preferred_element_type=jnp.float32
-            )
-            grad_user = part if grad_user is None else grad_user + part
-            cols = pl.ds(column * tile_size, tile_size)
-            grad_panel_ref[cols, :] += lax.dot_general(
-                errors, user_bf, (((0,), (0,)), ((), ())), preferred_element_type=jnp.float32
-            )
-        grad_user_ref[rows, :] = grad_user
+            part = scores[inner * tile_size : (inner + 1) * tile_size, column * tile_size : (column + 1) * tile_size]
+            row.append(((part - block) * live).astype(jnp.bfloat16))
+        pieces.append(jnp.concatenate(row, axis=1))
+    errors = jnp.concatenate(pieces, axis=0)
+    grad_user_ref[...] = jnp.dot(errors, panel_bf, preferred_element_type=jnp.float32)
+    grad_panel_ref[...] += lax.dot_general(
+        errors, user_bf, (((0,), (0,)), ((), ())), preferred_element_type=jnp.float32
+    )
 
 
 def local_grads(user_rows, panel_bf, codes, count, blocks, first):
@@ -84,21 +82,22 @@
         return pl.BlockSpec((None, tile_size, tile_size), index)
 
     rows = TILES_PER_STEP * tile_size
+    columns = item_tiles * tile_size
     grid_spec = pltpu.PrefetchScalarGridSpec(
         num_scalar_prefetch=2,
         grid=(user_tiles // TILES_PER_STEP,),
         in_specs=[
             pl.BlockSpec((rows, rank), lambda step, slot_ref, live_ref: (step, 0)),
-            pl.BlockSpec((item_tiles * tile_size, rank), lambda step, slot_ref, live_ref: (0, 0)),
+            pl.BlockSpec((columns, rank), lambda step, slot_ref, live_ref: (0, 0)),
         ]
         + [block_spec(inner, column) for inner in range(TILES_PER_STEP) for column in range(item_tiles)],
         out_specs=[
             pl.BlockSpec((rows, rank), lambda step, slot_ref, live_ref: (step, 0)),
-            pl.BlockSpec((item_tiles * tile_size, rank), lambda step, slot_ref, live_ref: (0, 0)),
+            pl.BlockSpec((columns, rank), lambda step, slot_ref, live_ref: (0, 0)),
         ],
     )
     flops = 3 * 2 * code_count * tile_size * tile_size * rank
-    moved_bytes = user_rows.size * 4 * 2 + panel_bf.size * 2 + code_count * tile_size * tile_size * 2 + panel_bf.size * 4
+    moved_bytes = user_rows.size * 8 + panel_bf.size * 6 + code_count * tile_size * tile_size * 2
     return pl.pallas_call(
         functools.partial(grads_kernel, item_tiles),
         grid_spec=grid_spec,

time: 146 us -> 116 us (0.79)
  Pallas kernels: 47.5 us -> 18 us
  waiting for transfers between devices: 63 us -> 48.7 us
  starting transfers between devices: 6.38 us -> 19.8 us
    pallas_call x2, Pallas kernels: 47.5 us -> 18 us  [local_grads(): pl.pallas_call(functools.partial(grads_kernel, item_tiles), grid_spec=gri...]
    ppermute x3, waiting for transfers between devices: 63 us -> 48.7 us  [branch(): return lambda held: lax.ppermute(held, 'user', pairs)]
    ppermute x3, starting transfers between devices: 6.3 us -> 19.6 us  [branch(): return lambda held: lax.ppermute(held, 'user', pairs)]
  transfers between devices with their start and end apart: 5 -> 5, of which waited for: 3 -> 3; matrix products, arithmetic and copies ran while one was open for 5% -> 6% of each run, Pallas kernels for 0% -> 0%
where the time goes in v3:
time: 116 us; the launch traced here: 115 us
  waiting for transfers between devices  48.7 us (42%)
  starting transfers between devices  19.8 us (17%)
  other arithmetic  18.6 us (16%)
  Pallas kernels  18 us (16%)
  local copies, waits for them, and re-layouts  6.48 us (6%)
  between operations  3.15 us (3%)
    ppermute x3, waiting for transfers between devices, branch(): return lambda held: lax.ppermute(held, 'user', pairs)  48.7 us
    ppermute x3, starting transfers between devices, branch(): return lambda held: lax.ppermute(held, 'user', pairs)  19.6 us
    pallas_call x2, Pallas kernels, local_grads(): pl.pallas_call(functools.partial(grads_kernel, item_tiles), grid_spec=gri...  18 us
    sub x2, other arithmetic, local(): user_rows - LEARNING_RATE * (grad_total + WEIGHT_DECAY * user_rows)  11.2 us
  transfers between devices with their start and end apart: 5, of which 3 were waited for; matrix products, arithmetic and copies ran while one was open for 6% of the time, Pallas kernels for 0%

profile of v3, /device:TPU:0, one launch (start us, length us, event | category | flops | bytes accessed | tf_op | source)
XLA Modules:
  0.0 114.8 jit_solution(8565673987846505783)
XLA Ops:
  0.6 1.0 copy.57
  1.7 0.8 slice_bitcast_fusion
  2.5 1.4 %fusion.5 = (s32[1,1,1]{2,1,0:T(1,128)}, s32[1,1,1]{2,1,0:T(1,128)}) fusion(s32[1,1,2]{2,1,0:T(1,128)} %param.34), kind=kLoop, calls=%fused_computation.25 | loop fusion | bytes 16 | tf_op jit(solution)/shard_map/slice | solution.py:123
  3.9 0.6 iota_compare_fusion.3
  4.5 0.1 fusion.1
  4.6 0.6 select_reduce_fusion.1.slot_ref
  5.2 1.3 %fusion.4 = (s32[1]{0:T(128)}, s32[1]{0:T(128)}) fusion(s32[2]{0:T(128)} %param.32), kind=kLoop, calls=%fused_computation.24 | loop fusion | bytes 16 | tf_op jit(solution)/shard_map/slice | solution.py:129
  6.6 0.5 convert_element_type.12.live_ref
  7.8 27.3 %conditional.5 = (f32[512,256]{1,0:T(8,128)S(1)}) conditional(s32[]{:T(128)} %bitcast.2, f32[512,256]{1,0:T(8,128)S(1)} %copy.57, f32[512,256]{1,0:T(8,128)S(1)} %copy.57, f32[512,256]{1,0:T(8,128)S(1)} %copy.57, f32[512,256]{1,0:T(8,128)S(1)} %copy.57, f32[512,256]{1,0:T(8,128)S(1)} %copy.57, ...), branch_computations={%region_2.0_spmd, %region_3.0_spmd, %region_4.0_spmd, %region_5.0_... | conditional | bytes 3145776 | solution.py:24
  7.8 4.1 %collective-permute-start.3 = (f32[512,256]{1,0:T(8,128)S(1)}, f32[512,256]{1,0:T(8,128)S(1)}, u32[]{:S(2)}, u32[]{:S(2)}) collective-permute-start(f32[512,256]{1,0:T(8,128)S(1)} %param.4), channel_id=1, source_target_pairs={{0,8},{2,10},{4,12},{6,14},{8,0},{10,2},{12,4},{14,6},{1,9},{3,11}... | collective-permute-start | bytes 1572872 | tf_op jit(solution)/shard_map/cond/branch_4_fun/ppermute | solution.py:22
  11.9 23.2 %collective-permute-done.3 = f32[512,256]{1,0:T(8,128)S(1)} collective-permute-done((f32[512,256]{1,0:T(8,128)S(1)}, f32[512,256]{1,0:T(8,128)S(1)}, u32[]{:S(2)}, u32[]{:S(2)}) %collective-permute-start.3) | collective-permute-done | bytes 524320 | tf_op jit(solution)/shard_map/cond/branch_4_fun/ppermute | solution.py:22
  35.1 0.7 convert_element_type.13.panel_ref
  35.8 8.9 %shard_map.101 = (f32[3072,256]{1,0:T(8,128)}, f32[512,256]{1,0:T(8,128)S(1)}) custom-call(s32[96]{0:T(128)} %select_reduce_fusion.1.slot_ref, s32[96]{0:T(128)} %convert_element_type.12.live_ref, f32[3072,256]{1,0:T(8,128)} %user_ref.1, bf16[512,256]{1,0:T(8,128)(2,1)} %convert_element_type.13.panel_ref, bf16[128,128,128]{2,1,0:T(8,128)(2,1)} %bitcast.25, ...), custom_call_target="tpu_custom_call" | custom-call | flops 2415919104 | bytes 10223616 | tf_op jit(solution)/shard_map/pallas_call | solution.py:101
  46.1 0.6 iota_compare_fusion.2
  46.7 0.1 fusion.3
  46.8 0.5 convert_element_type.14.live_ref
  47.3 18.6 %conditional.8 = (f32[512,256]{1,0:T(8,128)}, f32[512,256]{1,0:T(8,128)S(1)}) conditional(s32[]{:T(128)} %bitcast.6, (f32[512,256]{1,0:T(8,128)S(1)}, f32[512,256]{1,0:T(8,128)S(1)}, f32[512,256]{1,0:T(8,128)S(1)}) %tuple.164, (f32[512,256]{1,0:T(8,128)S(1)}, f32[512,256]{1,0:T(8,128)S(1)}, ...), branch_computations={%region_12.13_spmd, %region_13.14_spmd, %region_14.15_spmd, %regio... | conditional | flops 524288 | bytes 5242936
  47.4 0.1 multiply_subtract_fusion.7
  47.5 4.6 %collective-permute-start.20 = (f32[512,256]{1,0:T(8,128)S(1)}, f32[512,256]{1,0:T(8,128)}, u32[]{:S(2)}, u32[]{:S(2)}) collective-permute-start(f32[512,256]{1,0:T(8,128)S(1)} %multiply_subtract_fusion.7), channel_id=1, source_target_pairs={{0,14},{2,12},{4,10},{6,8},{8,6},{10,4},{12,2},{14,0},{1,15},{3,13... | collective-permute-start | bytes 1572872 | tf_op jit(solution)/shard_map/cond/branch_7_fun/ppermute | solution.py:22
  52.1 12.8 %collective-permute-done.20 = f32[512,256]{1,0:T(8,128)} collective-permute-done((f32[512,256]{1,0:T(8,128)S(1)}, f32[512,256]{1,0:T(8,128)}, u32[]{:S(2)}, u32[]{:S(2)}) %collective-permute-start.20) | collective-permute-done | bytes 524320 | tf_op jit(solution)/shard_map/cond/branch_7_fun/ppermute | solution.py:22
  64.9 1.0 copy.56
  65.9 0.7 convert_element_type.24.panel_ref
  66.6 0.1 select_reduce_fusion
  66.7 0.5 broadcast_add_fusion.slot_ref
  67.2 6.0 %multiply_subtract_fusion.9.user_ref = f32[3072,256]{1,0:T(8,128)} fusion(f32[3072,256]{1,0:T(8,128)} %user_ref.1, f32[3072,256]{1,0:T(8,128)} %get-tuple-element.186, f32[3072,256]{1,0:T(8,128)} %collective-permute-done.21), kind=kLoop, calls=%fused_computation.9 | loop fusion | flops 3932160 | bytes 12582912 | tf_op jit(solution)/shard_map/sub | solution.py:134
  73.3 9.1 %shard_map.102 = (f32[3072,256]{1,0:T(8,128)}, f32[512,256]{1,0:T(8,128)}) custom-call(s32[96]{0:T(128)} %broadcast_add_fusion.slot_ref, s32[96]{0:T(128)} %convert_element_type.14.live_ref, f32[3072,256]{1,0:T(8,128)} %multiply_subtract_fusion.9.user_ref, bf16[512,256]{1,0:T(8,128)(2,1)} %convert_element_type.24.panel_ref, bf16[128,128,128]{2,1,0:T(8,128)(2,1)} %bitcast.26, ...), custom_call_target="tpu_custom_call" | custom-call | flops 2415919104 | bytes 10223616 | tf_op jit(solution)/shard_map/pallas_call | solution.py:101
  83.1 2.1 %multiply_subtract_fusion.10 = f32[512,256]{1,0:T(8,128)} fusion(f32[512,256]{1,0:T(8,128)} %get-tuple-element.190, f32[512,256]{1,0:T(8,128)} %get-tuple-element.191), kind=kLoop, calls=%fused_computation.10 | loop fusion | flops 524288 | bytes 1572864 | tf_op jit(solution)/shard_map/sub | solution.py:127
  85.2 24.5 %conditional.7 = (f32[512,256]{1,0:T(8,128)}) conditional(s32[]{:T(128)} %bitcast.7, f32[512,256]{1,0:T(8,128)} %multiply_subtract_fusion.10, f32[512,256]{1,0:T(8,128)} %multiply_subtract_fusion.10, f32[512,256]{1,0:T(8,128)} %multiply_subtract_fusion.10, f32[512,256]{1,0:T(8,128)} %multiply_subtract_fusion.10, ...), branch_computations={%region_20.21_spmd, %region_21.22_spmd, %region_22.23_spmd, %regio... | conditional | bytes 3145776 | solution.py:24
  85.2 11.0 %collective-permute-start.9 = (f32[512,256]{1,0:T(8,128)}, f32[512,256]{1,0:T(8,128)S(1)}, u32[]{:S(2)}, u32[]{:S(2)}) collective-permute-start(f32[512,256]{1,0:T(8,128)} %param.19), channel_id=1, source_target_pairs={{0,6},{2,4},{4,2},{6,0},{8,14},{10,12},{12,10},{14,8},{1,7},{3,5},... | collective-permute-start | bytes 1572872 | tf_op jit(solution)/shard_map/cond/branch_3_fun/ppermute | solution.py:22
  96.1 12.8 %collective-permute-done.9 = f32[512,256]{1,0:T(8,128)S(1)} collective-permute-done((f32[512,256]{1,0:T(8,128)}, f32[512,256]{1,0:T(8,128)S(1)}, u32[]{:S(2)}, u32[]{:S(2)}) %collective-permute-start.9) | collective-permute-done | bytes 524320 | tf_op jit(solution)/shard_map/cond/branch_3_fun/ppermute | solution.py:22
  108.9 0.8 copy.35
  109.7 5.1 %multiply_subtract_fusion.8 = f32[3072,256]{1,0:T(8,128)} fusion(f32[3072,256]{1,0:T(8,128)S(1)} %copy-done, f32[3072,256]{1,0:T(8,128)} %get-tuple-element.189, f32[3072,256]{1,0:T(8,128)} %collective-permute-done.22), kind=kLoop, calls=%fused_computation.8 | loop fusion | flops 3932160 | bytes 12582912 | tf_op jit(solution)/shard_map/sub | solution.py:134
  (8 shorter events, 0.2 us)
Async XLA Ops:
  7.8 27.3 %collective-permute-start.3 = (f32[512,256]{1,0:T(8,128)S(1)}, f32[512,256]{1,0:T(8,128)S(1)}, u32[]{:S(2)}, u32[]{:S(2)}) collective-permute-start(f32[512,256]{1,0:T(8,128)S(1)} %param.4), channel_id=1, source_target_pairs={{0,8},{2,10},{4,12},{6,14},{8,0},{10,2},{12,4},{14,6},{1,9},{3,11}... | collective-permute-start | bytes 1572872 | tf_op jit(solution)/shard_map/cond/branch_4_fun/ppermute | solution.py:22
  44.8 22.5 %collective-permute-start.21 = (f32[3072,256]{1,0:T(8,128)}, f32[3072,256]{1,0:T(8,128)}, u32[]{:S(2)}, u32[]{:S(2)}) collective-permute-start(f32[3072,256]{1,0:T(8,128)} %get-tuple-element.186), channel_id=1, source_target_pairs={{0,1},{1,0},{2,3},{3,2},{4,5},{5,4},{6,7},{7,6},{8,9},{9,8},{10,11... | collective-permute-start | bytes 9437192 | tf_op jit(solution)/shard_map/ppermute | solution.py:29
  47.5 17.3 %collective-permute-start.20 = (f32[512,256]{1,0:T(8,128)S(1)}, f32[512,256]{1,0:T(8,128)}, u32[]{:S(2)}, u32[]{:S(2)}) collective-permute-start(f32[512,256]{1,0:T(8,128)S(1)} %multiply_subtract_fusion.7), channel_id=1, source_target_pairs={{0,14},{2,12},{4,10},{6,8},{8,6},{10,4},{12,2},{14,0},{1,15},{3,13... | collective-permute-start | bytes 1572872 | tf_op jit(solution)/shard_map/cond/branch_7_fun/ppermute | solution.py:22
  82.4 27.3 %collective-permute-start.22 = (f32[3072,256]{1,0:T(8,128)}, f32[3072,256]{1,0:T(8,128)}, u32[]{:S(2)}, u32[]{:S(2)}) collective-permute-start(f32[3072,256]{1,0:T(8,128)} %get-tuple-element.189), channel_id=1, source_target_pairs={{0,1},{1,0},{2,3},{3,2},{4,5},{5,4},{6,7},{7,6},{8,9},{9,8},{10,11... | collective-permute-start | bytes 9437192 | tf_op jit(solution)/shard_map/ppermute | solution.py:29
  85.2 24.6 %copy-start = (f32[3072,256]{1,0:T(8,128)S(1)}, f32[3072,256]{1,0:T(8,128)}, u32[]{:S(2)}) copy-start(f32[3072,256]{1,0:T(8,128)} %multiply_subtract_fusion.9.user_ref) | copy-start | bytes 9437188
  85.2 23.8 %collective-permute-start.9 = (f32[512,256]{1,0:T(8,128)}, f32[512,256]{1,0:T(8,128)S(1)}, u32[]{:S(2)}, u32[]{:S(2)}) collective-permute-start(f32[512,256]{1,0:T(8,128)} %param.19), channel_id=1, source_target_pairs={{0,6},{2,4},{4,2},{6,0},{8,14},{10,12},{12,10},{14,8},{1,7},{3,5},... | collective-permute-start | bytes 1572872 | tf_op jit(solution)/shard_map/cond/branch_3_fun/ppermute | solution.py:22

commit v4 on v3

--- a/solution.py
+++ b/solution.py
@@ -12,14 +12,18 @@
 TILES_PER_STEP = 4
 
 
-def moved(value, partner_mask):
+def moved(value, partner_mask, work):
     count = lax.axis_size("user")
 
     def branch(mask):
-        if mask == 0:
-            return lambda held: held
-        pairs = [(source, source ^ mask) for source in range(count)]
-        return lambda held: lax.ppermute(held, "user", pairs)
+        def run(held):
+            done = work()
+            if mask == 0:
+                return held, done
+            pairs = [(source, source ^ mask) for source in range(count)]
+            return lax.ppermute(held, "user", pairs), done
+
+        return run
 
     return lax.switch(partner_mask, [branch(mask) for mask in range(count)], value)
 
@@ -62,18 +66,23 @@
     )
 
 
-def local_grads(user_rows, panel_bf, codes, count, blocks, first):
-    tile_size = blocks.shape[-1]
-    rank = user_rows.shape[1]
-    user_tiles = user_rows.shape[0] // tile_size
-    item_tiles = panel_bf.shape[0] // tile_size
-    code_count = user_tiles * item_tiles
+def slot_tables(codes, count, first, code_count):
     slot_count = codes.shape[0]
     hits = (codes[:, None] == lax.iota(jnp.int32, code_count)[None, :]) & (
         lax.iota(jnp.int32, slot_count) < count
     )[:, None]
     live = jnp.any(hits, axis=0).astype(jnp.int32)
     slot_of = first + jnp.sum(jnp.where(hits, lax.iota(jnp.int32, slot_count)[:, None], 0), axis=0)
+    return slot_of, live
+
+
+def local_grads(user_rows, panel_bf, tables, blocks):
+    slot_of, live = tables
+    tile_size = blocks.shape[-1]
+    rank = user_rows.shape[1]
+    user_tiles = user_rows.shape[0] // tile_size
+    item_tiles = panel_bf.shape[0] // tile_size
+    code_count = user_tiles * item_tiles
 
     def block_spec(inner, column):
         def index(step, slot_ref, live_ref):
@@ -114,24 +123,31 @@
     stratum_total = stratum_masks.shape[0]
     slot_count = block_codes.shape[-1] // stratum_total
     tile_size = ratings.shape[-1]
+    code_count = (user_factors.shape[0] // tile_size) * (item_factors.shape[0] // tile_size)
     all_blocks = ratings.reshape(-1, tile_size, tile_size)
 
-    user_rows = user_factors
-    panel_now = moved(item_factors, stratum_masks[0])
-    for stratum in range(stratum_total):
+    def tables(stratum):
         codes = block_codes[0, 0, stratum * slot_count : (stratum + 1) * slot_count]
         count = block_counts[0, 0, stratum]
-        grad_user, grad_panel = local_grads(
-            user_rows, panel_now.astype(jnp.bfloat16), codes, count, all_blocks, stratum * slot_count
-        )
+        return slot_tables(codes, count, stratum * slot_count, code_count)
+
+    user_rows = user_factors
+    panel_now, ready = moved(item_factors, stratum_masks[0], lambda: tables(0))
+    for stratum in range(stratum_total):
+        grad_user, grad_panel = local_grads(user_rows, panel_now.astype(jnp.bfloat16), ready, all_blocks)
         panel_next = panel_now - LEARNING_RATE * (grad_panel + WEIGHT_DECAY * panel_now)
-        if stratum + 1 < stratum_total:
+        last = stratum + 1 == stratum_total
+        if last:
+            step_mask = stratum_masks[stratum]
+        else:
             step_mask = jnp.bitwise_xor(stratum_masks[stratum], stratum_masks[stratum + 1])
-        else:
-            step_mask = stratum_masks[stratum]
-        panel_now = moved(panel_next, step_mask)
-        grad_total = item_sum(grad_user)
-        user_rows = user_rows - LEARNING_RATE * (grad_total + WEIGHT_DECAY * user_rows)
+
+        def user_step(grad_user=grad_user, user_rows=user_rows, last=last, stratum=stratum):
+            grad_total = item_sum(grad_user)
+            rows = user_rows - LEARNING_RATE * (grad_total + WEIGHT_DECAY * user_rows)
+            return rows, (None if last else tables(stratum + 1))
+
+        panel_now, (user_rows, ready) = moved(panel_next, step_mask, user_step)
     return (user_rows, panel_now)
 
 

time: 116 us -> 111 us (0.957)
  waiting for transfers between devices: 48.7 us -> 44.7 us
  starting transfers between devices: 19.8 us -> 17.1 us
  local copies, waits for them, and re-layouts: 6.48 us -> 8.88 us
  other arithmetic: 18.6 us -> 17.3 us
    ppermute x3, waiting for transfers between devices: 48.7 us -> 44.6 us  [run(): return (lax.ppermute(held, 'user', pairs), done)]
    ppermute x3, starting transfers between devices: 19.6 us -> 17 us  [run(): return (lax.ppermute(held, 'user', pairs), done)]
    sub x2, other arithmetic: 2.19 us -> 4 us  [local(): panel_now - LEARNING_RATE * (grad_panel + WEIGHT_DECAY * panel_now)]
    unnamed x4 -> x11, local copies, waits for them, and re-layouts: 2.09 us -> 3.74 us
    sub x2, other arithmetic: 11.2 us -> 9.89 us  [user_step(): rows = user_rows - LEARNING_RATE * (grad_total + WEIGHT_DECAY * user_rows)]
  transfers between devices with their start and end apart: 5 -> 5, of which waited for: 3 -> 3; matrix products, arithmetic and copies ran while one was open for 6% -> 9% of each run, Pallas kernels for 0% -> 0%
where the time goes in v4:
time: 111 us; the launch traced here: 109 us
  waiting for transfers between devices  44.7 us (40%)
  Pallas kernels  17.5 us (16%)
  other arithmetic  17.3 us (16%)
  starting transfers between devices  17.1 us (15%)
  local copies, waits for them, and re-layouts  8.88 us (8%)
  between operations  3.26 us (3%)
    ppermute x3, waiting for transfers between devices, run(): return (lax.ppermute(held, 'user', pairs), done)  44.6 us
    pallas_call x2, Pallas kernels, local_grads(): pl.pallas_call(functools.partial(grads_kernel, item_tiles), grid_spec=gri...  17.5 us
    ppermute x3, starting transfers between devices, run(): return (lax.ppermute(held, 'user', pairs), done)  17 us
    sub x2, other arithmetic, user_step(): rows = user_rows - LEARNING_RATE * (grad_total + WEIGHT_DECAY * user_rows)  9.89 us
    sub x2, other arithmetic, local(): panel_now - LEARNING_RATE * (grad_panel + WEIGHT_DECAY * panel_now)  4 us
    unnamed x11, local copies, waits for them, and re-layouts  3.74 us
  transfers between devices with their start and end apart: 5, of which 3 were waited for; matrix products, arithmetic and copies ran while one was open for 9% of the time, Pallas kernels for 0%

profile of v4, /device:TPU:0, one launch (start us, length us, event | category | flops | bytes accessed | tf_op | source)
XLA Modules:
  0.0 109.1 jit_solution(15959273190913422695)
XLA Ops:
  0.6 1.0 copy.98
  1.7 1.3 %fusion.33 = (s32[1]{0:T(128)}, s32[1]{0:T(128)}) fusion(s32[2]{0:T(128)} %param.32), kind=kLoop, calls=%fused_computation.130 | loop fusion | bytes 16 | tf_op jit(solution)/shard_map/slice | solution.py:143
  5.6 17.2 %conditional.10 = (f32[512,256]{1,0:T(8,128)S(1)}, s32[96]{0:T(128)S(1)}, s32[96]{0:T(128)S(1)}) conditional(s32[]{:T(128)} %bitcast.34, (s32[1,1,128]{2,1,0:T(1,128)}, s32[1,1,2]{2,1,0:T(1,128)}, f32[512,256]{1,0:T(8,128)S(1)}) %tuple.189, (f32[512,256]{1,0:T(8,128)S(1)}, s32[1,1,128]{2,1,0:T(1,128)}, ...), branch_computations={%region_0.3_spmd, %region_3.6_spmd, %region_6.9_spmd, %region_9.12... | conditional | flops 42976 | bytes 3147972
  5.6 5.1 %collective-permute-start.5 = (f32[512,256]{1,0:T(8,128)S(1)}, f32[512,256]{1,0:T(8,128)S(1)}, u32[]{:S(2)}, u32[]{:S(2)}) collective-permute-start(f32[512,256]{1,0:T(8,128)S(1)} %get-tuple-element.399), channel_id=1, source_target_pairs={{0,12},{2,14},{4,8},{6,10},{8,4},{10,6},{12,0},{14,2},{1,13},{3,15... | collective-permute-start | bytes 1572872 | tf_op jit(solution)/shard_map/cond/branch_6_fun/ppermute | solution.py:24
  10.7 0.6 iota_compare_fusion.13
  11.4 0.7 slice_bitcast_fusion.6
  12.0 0.1 fusion.13
  12.2 0.1 select_reduce_fusion.6
  12.3 10.5 %collective-permute-done.5 = f32[512,256]{1,0:T(8,128)S(1)} collective-permute-done((f32[512,256]{1,0:T(8,128)S(1)}, f32[512,256]{1,0:T(8,128)S(1)}, u32[]{:S(2)}, u32[]{:S(2)}) %collective-permute-start.5) | collective-permute-done | bytes 524320 | tf_op jit(solution)/shard_map/cond/branch_6_fun/ppermute | solution.py:24
  22.8 0.8 copy-done.8
  23.6 0.7 convert_element_type.104.panel_ref
  24.3 9.0 %shard_map.77 = (f32[3072,256]{1,0:T(8,128)S(1)}, f32[512,256]{1,0:T(8,128)}) custom-call(s32[96]{0:T(128)S(1)} %get-tuple-element.520.slot_ref, s32[96]{0:T(128)S(1)} %get-tuple-element.546.live_ref, f32[3072,256]{1,0:T(8,128)} %user_ref.1, bf16[512,256]{1,0:T(8,128)(2,1)} %convert_element_type.104.panel_ref, bf16[128,128,128]{2,1,0:T(8,128)(2,1)} %bitcast.75, ...), custom_call_target="tpu_custom_call" | custom-call | flops 2415919104 | bytes 10223616 | tf_op jit(solution)/shard_map/pallas_call | solution.py:110
  33.3 0.8 broadcast.210
  34.1 42.4 %conditional.11 = (f32[512,256]{1,0:T(8,128)}, f32[3072,256]{1,0:T(8,128)S(1)}, s32[96]{0:T(128)S(1)}, bf16[512,256]{1,0:T(8,128)(2,1)S(1)}, s32[96]{0:T(128)S(1)}) conditional(s32[]{:T(128)} %bitcast.33, (f32[512,256]{1,0:T(8,128)}, f32[512,256]{1,0:T(8,128)}, f32[512,256]{1,0:T(8,128)}, f32[3072,256]{1,0:T(8,128)S(1)}, ...), branch_computations={%region_24.27_spmd, %region_27.30_spmd, %region_30.33_spmd, %regio... | conditional | flops 4630592 | bytes 42732576
  34.2 2.5 %multiply_subtract_fusion.9 = f32[512,256]{1,0:T(8,128)S(1)} fusion(f32[512,256]{1,0:T(8,128)} %get-tuple-element.433, f32[512,256]{1,0:T(8,128)} %get-tuple-element.435, f32[512,256]{1,0:T(8,128)} %get-tuple-element.434), kind=kLoop, calls=%fused_computation.85 | loop fusion | flops 524288 | bytes 2097152 | tf_op jit(solution)/shard_map/sub | solution.py:138
  36.8 11.8 %collective-permute-start.13 = (f32[512,256]{1,0:T(8,128)S(1)}, f32[512,256]{1,0:T(8,128)}, u32[]{:S(2)}, u32[]{:S(2)}) collective-permute-start(f32[512,256]{1,0:T(8,128)S(1)} %multiply_subtract_fusion.9), channel_id=1, source_target_pairs={{0,8},{2,10},{4,12},{6,14},{8,0},{10,2},{12,4},{14,6},{1,9},{3,11}... | collective-permute-start | bytes 1572872 | tf_op jit(solution)/shard_map/cond/branch_4_fun/ppermute | solution.py:24
  48.6 0.6 slice.95
  49.2 0.6 iota_compare_fusion.25
  49.8 0.1 fusion.25
  49.9 0.1 select_reduce_fusion.12
  50.0 21.4 %collective-permute-done.13 = f32[512,256]{1,0:T(8,128)} collective-permute-done((f32[512,256]{1,0:T(8,128)S(1)}, f32[512,256]{1,0:T(8,128)}, u32[]{:S(2)}, u32[]{:S(2)}) %collective-permute-start.13) | collective-permute-done | bytes 524320 | tf_op jit(solution)/shard_map/cond/branch_4_fun/ppermute | solution.py:24
  71.4 1.1 convert_element_type.120
  72.5 3.9 %multiply_subtract_fusion.8 = f32[3072,256]{1,0:T(8,128)S(1)} fusion(f32[3072,256]{1,0:T(8,128)} %get-tuple-element.436, f32[3072,256]{1,0:T(8,128)} %copy-done.4, f32[3072,256]{1,0:T(8,128)S(1)} %collective-permute-done.14), kind=kLoop, calls=%fused_computation.84 | loop fusion | flops 3932160 | bytes 12582912 | tf_op jit(solution)/shard_map/cond/branch_4_fun/sub | solution.py:147
  76.6 8.5 %shard_map.78 = (f32[3072,256]{1,0:T(8,128)}, f32[512,256]{1,0:T(8,128)}) custom-call(s32[96]{0:T(128)S(1)} %get-tuple-element.525.slot_ref, s32[96]{0:T(128)S(1)} %get-tuple-element.548.live_ref, f32[3072,256]{1,0:T(8,128)S(1)} %get-tuple-element.527.user_ref, bf16[512,256]{1,0:T(8,128)(2,1)S(1)} %get-tuple-element.547.panel_ref, ...), custom_call_target="tpu_custom_call" | custom-call | flops 2415919104 | bytes 10223616 | tf_op jit(solution)/shard_map/pallas_call | solution.py:110
  85.1 16.1 %conditional.9 = (f32[512,256]{1,0:T(8,128)}, f32[3072,256]{1,0:T(8,128)S(1)}, f32[3072,256]{1,0:T(8,128)}, f32[3072,256]{1,0:T(8,128)}, f32[3072,256]{1,0:T(8,128)}, /*index=5*/f32[3072,256]{1,0:T(8,128)}) conditional(s32[]{:T(128)} %bitcast.32, (f32[512,256]{1,0:T(8,128)}, f32[512,256]{1,0:T(8,128)}, ...), branch_computations={%region_48.49_spmd, %region_49.50_spmd, %region_50.51_spmd, %regio... | conditional | flops 524288 | bytes 23068800 | solution.py:28
  85.1 0.1 collective-permute-start.25
  85.2 1.5 %multiply_subtract_fusion.18 = f32[512,256]{1,0:T(8,128)S(1)} fusion(f32[512,256]{1,0:T(8,128)} %get-tuple-element.471, f32[512,256]{1,0:T(8,128)} %get-tuple-element.473, f32[512,256]{1,0:T(8,128)} %get-tuple-element.472), kind=kLoop, calls=%fused_computation.122 | loop fusion | flops 524288 | bytes 2097152 | tf_op jit(solution)/shard_map/sub | solution.py:138
  86.7 0.1 collective-permute-start.24
  86.8 1.7 %copy.90 = f32[3072,256]{1,0:T(8,128)} copy(f32[3072,256]{1,0:T(8,128)S(1)} %get-tuple-element.679) | data formatting | bytes 6291456 | tf_op jit(solution)/shard_map/cond
  88.4 12.7 %collective-permute-done.24 = f32[512,256]{1,0:T(8,128)} collective-permute-done((f32[512,256]{1,0:T(8,128)S(1)}, f32[512,256]{1,0:T(8,128)}, u32[]{:S(2)}, u32[]{:S(2)}) %collective-permute-start.24) | collective-permute-done | bytes 524320 | tf_op jit(solution)/shard_map/cond/branch_2_fun/ppermute | solution.py:24
  101.2 6.0 %multiply_subtract_fusion.24 = f32[3072,256]{1,0:T(8,128)} fusion(f32[3072,256]{1,0:T(8,128)} %get-tuple-element.531, f32[3072,256]{1,0:T(8,128)} %get-tuple-element.532, f32[3072,256]{1,0:T(8,128)} %get-tuple-element.533), kind=kLoop, calls=%fused_computation.128 | loop fusion | flops 3932160 | bytes 12582912 | tf_op jit(solution)/shard_map/cond/branch_0_fun/sub | solution.py:147
  107.2 1.9 %copy.99 = f32[512,256]{1,0:T(8,128)} copy(f32[512,256]{1,0:T(8,128)} %get-tuple-element.716) | data formatting | bytes 1048576
  (15 shorter events, 0.2 us)
Async XLA Ops:
  5.6 17.1 %collective-permute-start.5 = (f32[512,256]{1,0:T(8,128)S(1)}, f32[512,256]{1,0:T(8,128)S(1)}, u32[]{:S(2)}, u32[]{:S(2)}) collective-permute-start(f32[512,256]{1,0:T(8,128)S(1)} %get-tuple-element.399), channel_id=1, source_target_pairs={{0,12},{2,14},{4,8},{6,10},{8,4},{10,6},{12,0},{14,2},{1,13},{3,15... | collective-permute-start | bytes 1572872 | tf_op jit(solution)/shard_map/cond/branch_6_fun/ppermute | solution.py:24
  22.8 0.8 copy-start.8
  24.3 9.8 %copy-start.10 = (s32[1,1,128]{2,1,0:T(1,128)S(1)}, s32[1,1,128]{2,1,0:T(1,128)}, u32[]{:S(2)}) copy-start(s32[1,1,128]{2,1,0:T(1,128)} %param.33) | copy-start | bytes 1540
  24.3 9.8 %copy-start.11 = (s32[1,1,2]{2,1,0:T(1,128)S(1)}, s32[1,1,2]{2,1,0:T(1,128)}, u32[]{:S(2)}) copy-start(s32[1,1,2]{2,1,0:T(1,128)} %param.34) | copy-start | bytes 28
  34.1 38.4 %copy-start.4 = (f32[3072,256]{1,0:T(8,128)}, f32[3072,256]{1,0:T(8,128)S(1)}, u32[]{:S(2)}) copy-start(f32[3072,256]{1,0:T(8,128)S(1)} %get-tuple-element.437) | copy-start | bytes 9437188
  34.1 38.3 %collective-permute-start.14 = (f32[3072,256]{1,0:T(8,128)S(1)}, f32[3072,256]{1,0:T(8,128)S(1)}, u32[]{:S(2)}, u32[]{:S(2)}) collective-permute-start(f32[3072,256]{1,0:T(8,128)S(1)} %get-tuple-element.437), channel_id=1, source_target_pairs={{0,1},{1,0},{2,3},{3,2},{4,5},{5,4},{6,7},{7,6},{8,9},{9,8},{10,11... | collective-permute-start | bytes 9437192 | tf_op jit(solution)/shard_map/cond/branch_4_fun/ppermute | solution.py:33
  36.8 34.7 %collective-permute-start.13 = (f32[512,256]{1,0:T(8,128)S(1)}, f32[512,256]{1,0:T(8,128)}, u32[]{:S(2)}, u32[]{:S(2)}) collective-permute-start(f32[512,256]{1,0:T(8,128)S(1)} %multiply_subtract_fusion.9), channel_id=1, source_target_pairs={{0,8},{2,10},{4,12},{6,14},{8,0},{10,2},{12,4},{14,6},{1,9},{3,11}... | collective-permute-start | bytes 1572872 | tf_op jit(solution)/shard_map/cond/branch_4_fun/ppermute | solution.py:24
  85.1 16.0 %collective-permute-start.25 = (f32[3072,256]{1,0:T(8,128)}, f32[3072,256]{1,0:T(8,128)}, u32[]{:S(2)}, u32[]{:S(2)}) collective-permute-start(f32[3072,256]{1,0:T(8,128)} %get-tuple-element.681), channel_id=1, source_target_pairs={{0,1},{1,0},{2,3},{3,2},{4,5},{5,4},{6,7},{7,6},{8,9},{9,8},{10,11... | collective-permute-start | bytes 9437192 | tf_op jit(solution)/shard_map/cond/branch_2_fun/ppermute | solution.py:33
  86.7 14.5 %collective-permute-start.24 = (f32[512,256]{1,0:T(8,128)S(1)}, f32[512,256]{1,0:T(8,128)}, u32[]{:S(2)}, u32[]{:S(2)}) collective-permute-start(f32[512,256]{1,0:T(8,128)S(1)} %multiply_subtract_fusion.18), channel_id=1, source_target_pairs={{0,4},{2,6},{4,0},{6,2},{8,12},{10,14},{12,8},{14,10},{1,5},{3,7},... | collective-permute-start | bytes 1572872 | tf_op jit(solution)/shard_map/cond/branch_2_fun/ppermute | solution.py:24

commit v5 on v4

v5 whole, which is shorter than its diff:
```python
import functools

import jax
import jax.numpy as jnp
from jax import lax
from jax.experimental import pallas as pl
from jax.experimental.pallas import tpu as pltpu
from jax.sharding import PartitionSpec as P

LEARNING_RATE = 0.02
WEIGHT_DECAY = 0.1
TILES_PER_STEP = 4


def moved(value, partner_mask, work):
    count = lax.axis_size("user")

    def branch(mask):
        def run(held):
            done = work()
            if mask == 0:
                return held, done
            pairs = [(source, source ^ mask) for source in range(count)]
            return lax.ppermute(held, "user", pairs), done

        return run

    return lax.switch(partner_mask, [branch(mask) for mask in range(count)], value)


def item_sum(value):
    if lax.axis_size("item") == 2:
        return value + lax.ppermute(value, "item", [(0, 1), (1, 0)])
    return lax.psum(value, "item")


def grads_kernel(item_tiles, code_stride, offset, summed, slot_ref, live_ref, user_ref, panel_ref, *rest):
    block_refs = rest[: TILES_PER_STEP * item_tiles]
    rest = rest[TILES_PER_STEP * item_tiles :]
    earlier_ref = rest[0] if summed else None
    grad_user_ref, grad_panel_ref = rest[1:] if summed else rest
    step = pl.program_id(0)
    tile_size = block_refs[0].shape[-1]

    @pl.when(step == 0)
    def _():
        grad_panel_ref[...] = jnp.zeros_like(grad_panel_ref)

    user_bf = user_ref[...].astype(jnp.bfloat16)
    panel_bf = panel_ref[...]
    scores = lax.dot_general(
        user_bf, panel_bf, (((1,), (1,)), ((), ())), preferred_element_type=jnp.float32
    )
    pieces = []
    for inner in range(TILES_PER_STEP):
        row = []
        for column in range(item_tiles):
            code = (step * TILES_PER_STEP + inner) * code_stride + offset + column
            live = live_ref[code].astype(jnp.float32)
            block = block_refs[inner * item_tiles + column][...].astype(jnp.float32)
            part = scores[inner * tile_size : (inner + 1) * tile_size, column * tile_size : (column + 1) * tile_size]
            row.append(((part - block) * live).astype(jnp.bfloat16))
        pieces.append(jnp.concatenate(row, axis=1))
    errors = jnp.concatenate(pieces, axis=0)
    grad_user = jnp.dot(errors, panel_bf, preferred_element_type=jnp.float32)
    grad_user_ref[...] = grad_user + earlier_ref[...] if summed else grad_user
    grad_panel_ref[...] += lax.dot_general(
        errors, user_bf, (((0,), (0,)), ((), ())), preferred_element_type=jnp.float32
    )


def slot_tables(codes, count, first, code_count):
    slot_count = codes.shape[0]
    hits = (codes[:, None] == lax.iota(jnp.int32, code_count)[None, :]) & (
        lax.iota(jnp.int32, slot_count) < count
    )[:, None]
    live = jnp.any(hits, axis=0).astype(jnp.int32)
    slot_of = first + jnp.sum(jnp.where(hits, lax.iota(jnp.int32, slot_count)[:, None], 0), axis=0)
    return slot_of, live


def local_grads(user_rows, panel_bf, tables, blocks, code_stride, offset, earlier=None):
    slot_of, live = tables
    tile_size = blocks.shape[-1]
    rank = user_rows.shape[1]
    user_tiles = user_rows.shape[0] // tile_size
    item_tiles = panel_bf.shape[0] // tile_size
    code_count = user_tiles * item_tiles
    summed = earlier is not None

    def block_spec(inner, column):
        def index(step, slot_ref, live_ref):
            return (slot_ref[(step * TILES_PER_STEP + inner) * code_stride + offset + column], 0, 0)

        return pl.BlockSpec((None, tile_size, tile_size), index)

    rows = TILES_PER_STEP * tile_size
    columns = item_tiles * tile_size
    user_spec = pl.BlockSpec((rows, rank), lambda step, slot_ref, live_ref: (step, 0))
    grid_spec = pltpu.PrefetchScalarGridSpec(
        num_scalar_prefetch=2,
        grid=(user_tiles // TILES_PER_STEP,),
        in_specs=[user_spec, pl.BlockSpec((columns, rank), lambda step, slot_ref, live_ref: (0, 0))]
        + [block_spec(inner, column) for inner in range(TILES_PER_STEP) for column in range(item_tiles)]
        + ([user_spec] if summed else []),
        out_specs=[user_spec, pl.BlockSpec((columns, rank), lambda step, slot_ref, live_ref: (0, 0))],
    )
    flops = 3 * 2 * code_count * tile_size * tile_size * rank
    moved_bytes = user_rows.size * (12 if summed else 8) + panel_bf.size * 6 + code_count * tile_size * tile_size * 2
    operands = [slot_of, live, user_rows, panel_bf] + [blocks] * (TILES_PER_STEP * item_tiles)
    return pl.pallas_call(
        functools.partial(grads_kernel, item_tiles, code_stride, offset, summed),
        grid_spec=grid_spec,
        out_shape=[
            jax.ShapeDtypeStruct(user_rows.shape, jnp.float32),
            jax.ShapeDtypeStruct(panel_bf.shape, jnp.float32),
        ],
        input_output_aliases={len(operands): 0} if summed else {},
        compiler_params=pltpu.CompilerParams(dimension_semantics=("arbitrary",)),
        cost_estimate=pl.CostEstimate(flops=flops, bytes_accessed=moved_bytes, transcendentals=0),
    )(*operands, *([earlier] if summed else []))


def local(user_factors, item_factors, stratum_masks, block_codes, block_counts, ratings):
    stratum_total = stratum_masks.shape[0]
    slot_count = block_codes.shape[-1] // stratum_total
    tile_size = ratings.shape[-1]
    item_tiles = item_factors.shape[0] // tile_size
    code_count = (user_factors.shape[0] // tile_size) * item_tiles
    all_blocks = ratings.reshape(-1, tile_size, tile_size)
    half_tiles = item_tiles // 2
    half_rows = half_tiles * tile_size

    def tables(stratum):
        codes = block_codes[0, 0, stratum * slot_count : (stratum + 1) * slot_count]
        count = block_counts[0, 0, stratum]
        return slot_tables(codes, count, stratum * slot_count, code_count)

    def half_step(user_rows, panel_half, ready, half, earlier):
        grad_user, grad_panel = local_grads(
            user_rows, panel_half.astype(jnp.bfloat16), ready, all_blocks, item_tiles, half * half_tiles, earlier
        )
        return grad_user, panel_half - LEARNING_RATE * (grad_panel + WEIGHT_DECAY * panel_half)

    def step_mask(stratum):
        if stratum + 1 == stratum_total:
            return stratum_masks[stratum]
        return jnp.bitwise_xor(stratum_masks[stratum], stratum_masks[stratum + 1])

    first_half, ready = moved(item_factors[:half_rows], stratum_masks[0], lambda: tables(0))
    user_rows = user_factors
    grad_user = None
    done_first = None
    second_in = item_factors[half_rows:]
    second_mask = stratum_masks[0]
    for stratum in range(stratum_total):
        last = stratum + 1 == stratum_total
        if done_first is None:
            second_half, (grad_user, done_first) = moved(
                second_in, second_mask,
                lambda: half_step(user_rows, first_half, ready, 0, None),
            )
        out_first, (grad_user, done_second) = moved(
            done_first, step_mask(stratum),
            lambda: half_step(user_rows, second_half, ready, 1, grad_user),
        )

        def user_step(grad_user=grad_user, user_rows=user_rows, last=last, stratum=stratum, out_first=out_first):
            grad_total = item_sum(grad_user)
            rows = user_rows - LEARNING_RATE * (grad_total + WEIGHT_DECAY * user_rows)
            if last:
                return rows, None, None, None
            ready_next = tables(stratum + 1)
            grad_next, first_next = half_step(rows, out_first, ready_next, 0, None)
            return rows, ready_next, grad_next, first_next

        out_second, (user_rows, ready, grad_user, done_first) = moved(done_second, step_mask(stratum), user_step)
        first_half, second_half = out_first, out_second
    return (user_rows, jnp.concatenate([first_half, second_half], axis=0))


def solution(mesh):
    placed = (
        P(("groups", "user"), None),
        P(("groups", "user", "item"), None),
        P("groups"),
        P(("groups", "user"), "item", None),
        P(("groups", "user"), "item", None),
        P(("groups", "user"), "item", None, None, None),
    )
    return jax.shard_map(
        local,
        mesh=mesh,
        in_specs=placed,
        out_specs=(P(("groups", "user"), None), P(("groups", "user", "item"), None)),
        check_vma=False,
    )
```

time: 111 us -> 119 us (1.072)
  Pallas kernels: 17.5 us -> 29.1 us
  waiting for transfers between devices: 44.7 us -> 33.5 us
  starting transfers between devices: 17.1 us -> 7.22 us
  other arithmetic: 17.3 us -> 25.8 us
  local copies, waits for them, and re-layouts: 8.88 us -> 17 us
    pallas_call x2 -> x4, Pallas kernels: 17.5 us -> 29.1 us  [local_grads(): pl.pallas_call(functools.partial(grads_kernel, item_tiles, code_stride, o...]
    ppermute x3 -> x6, waiting for transfers between devices: 44.6 us -> 33.5 us  [run(): return (lax.ppermute(held, 'user', pairs), done)]
    ppermute x3 -> x6, starting transfers between devices: 17 us -> 7.15 us  [run(): return (lax.ppermute(held, 'user', pairs), done)]
    cond x1 -> x9, local copies, waits for them, and re-layouts: 1.67 us -> 11.1 us
    convert_element_type x2 -> x4, other arithmetic: 1.8 us -> 5.5 us  [half_step(): panel_half.astype(jnp.bfloat16)]
    unnamed x11 -> x8, local copies, waits for them, and re-layouts: 3.74 us -> 1.42 us
    sub x2 -> x4, other arithmetic: 4 us -> 6 us  [half_step(): panel_half - LEARNING_RATE * (grad_panel + WEIGHT_DECAY * panel_half)]
    slice x1 -> x2, local copies, waits for them, and re-layouts: 1.31 us -> 3.17 us  [the longest x1 1.77 us: local(): second_in = item_factors[half_rows:]]
  transfers between devices with their start and end apart: 5 -> 8, of which waited for: 3 -> 5; matrix products, arithmetic and copies ran while one was open for 9% -> 17% of each run, Pallas kernels for 0% -> 19%
where the time goes in v5:
time: 119 us; the launch traced here: 117 us
  waiting for transfers between devices  33.5 us (28%)
  Pallas kernels  29.1 us (24%)
  other arithmetic  25.8 us (22%)
  local copies, waits for them, and re-layouts  17 us (14%)
  starting transfers between devices  7.22 us (6%)
  between operations  3.46 us (3%)
    ppermute x6, waiting for transfers between devices, run(): return (lax.ppermute(held, 'user', pairs), done)  33.5 us
    pallas_call x4, Pallas kernels, local_grads(): pl.pallas_call(functools.partial(grads_kernel, item_tiles, code_stride, o...  29.1 us
    cond x9, local copies, waits for them, and re-layouts  11.1 us
    sub x2, other arithmetic, user_step(): rows = user_rows - LEARNING_RATE * (grad_total + WEIGHT_DECAY * user_rows)  9.65 us
    ppermute x6, starting transfers between devices, run(): return (lax.ppermute(held, 'user', pairs), done)  7.15 us
    sub x4, other arithmetic, half_step(): panel_half - LEARNING_RATE * (grad_panel + WEIGHT_DECAY * panel_half)  6 us
    convert_element_type x4, other arithmetic, half_step(): panel_half.astype(jnp.bfloat16)  5.5 us
  transfers between devices with their start and end apart: 8, of which 5 were waited for; matrix products, arithmetic and copies ran while one was open for 17% of the time, Pallas kernels for 19%

profile of v5, /device:TPU:0, one launch (start us, length us, event | category | flops | bytes accessed | tf_op | source)
XLA Modules:
  0.0 116.7 jit_solution(10849654021930764761)
XLA Ops:
  0.6 1.4 %fusion.33 = (s32[1]{0:T(128)}, s32[1]{0:T(128)}) fusion(s32[2]{0:T(128)} %param.56), kind=kLoop, calls=%fused_computation.140 | loop fusion | bytes 16 | tf_op jit(solution)/shard_map/slice | solution.py:148
  4.6 1.8 %fusion.32 = (f32[256,256]{1,0:T(8,128)S(1)}, f32[256,256]{1,0:T(8,128)}) fusion(f32[512,256]{1,0:T(8,128)} %param.55), kind=kLoop, calls=%fused_computation.139 | loop fusion | bytes 1048576 | tf_op jit(solution)/shard_map/slice | solution.py:154
  6.4 17.8 %conditional.16 = (f32[256,256]{1,0:T(8,128)}, s32[96]{0:T(128)S(1)}, s32[96]{0:T(128)S(1)}) conditional(s32[]{:T(128)} %bitcast.34, (s32[1,1,128]{2,1,0:T(1,128)}, s32[1,1,2]{2,1,0:T(1,128)}, f32[256,256]{1,0:T(8,128)}) %tuple.286, (f32[256,256]{1,0:T(8,128)}, s32[1,1,128]{2,1,0:T(1,128)}, ...), branch_computations={%region_0.3_spmd, %region_3.6_spmd, %region_6.9_spmd, %region_9.12... | conditional | flops 42976 | bytes 1575108
  6.4 5.0 %collective-permute-start.26 = (f32[256,256]{1,0:T(8,128)}, f32[256,256]{1,0:T(8,128)S(1)}, u32[]{:S(2)}, u32[]{:S(2)}) collective-permute-start(f32[256,256]{1,0:T(8,128)} %get-tuple-element.580), channel_id=1, source_target_pairs={{0,10},{2,8},{4,14},{6,12},{8,2},{10,0},{12,6},{14,4},{1,11},{3,9}... | collective-permute-start | bytes 786440 | tf_op jit(solution)/shard_map/cond/branch_5_fun/ppermute | solution.py:24
  12.9 10.6 %collective-permute-done.26 = f32[256,256]{1,0:T(8,128)S(1)} collective-permute-done((f32[256,256]{1,0:T(8,128)}, f32[256,256]{1,0:T(8,128)S(1)}, u32[]{:S(2)}, u32[]{:S(2)}) %collective-permute-start.26) | collective-permute-done | bytes 262176 | tf_op jit(solution)/shard_map/cond/branch_5_fun/ppermute | solution.py:24
  24.2 16.0 %conditional.11 = (f32[256,256]{1,0:T(8,128)S(1)}, f32[3072,256]{1,0:T(8,128)}, f32[256,256]{1,0:T(8,128)}) conditional(s32[]{:T(128)} %bitcast.34, (f32[256,256]{1,0:T(8,128)}, s32[96]{0:T(128)S(1)}, s32[96]{0:T(128)S(1)}, f32[3072,256]{1,0:T(8,128)S(1)}, bf16[128,128,128]{2,1,0:T(8,128)(2,1)}, ...), branch_computations={%region_24.25_spmd, %region_25.26_spmd, %region_26.27_spmd, %regio... | conditional | flops 1208287232 | bytes 11010112 | solution.py:28
  24.2 1.6 %convert_element_type.127.panel_ref = bf16[256,256]{1,0:T(8,128)(2,1)} convert(f32[256,256]{1,0:T(8,128)} %get-tuple-element.633) | non-fusion elementwise | flops 65536 | bytes 393216 | tf_op jit(solution)/shard_map/cond/branch_5_fun/convert_element_type | solution.py:141
  25.8 6.7 %branch_5_fun.4 = (f32[3072,256]{1,0:T(8,128)}, f32[256,256]{1,0:T(8,128)}) custom-call(s32[96]{0:T(128)S(1)} %get-tuple-element.630.slot_ref, s32[96]{0:T(128)S(1)} %get-tuple-element.631.live_ref, f32[3072,256]{1,0:T(8,128)S(1)} %get-tuple-element.632.user_ref, bf16[256,256]{1,0:T(8,128)(2,1)} %convert_element_type.127.panel_ref, ...), custom_call_target="tpu_custom_call" | custom-call | flops 1207959552 | bytes 8257536 | tf_op jit(solution)/shard_map/cond/branch_5_fun/pallas_call | solution.py:111
  32.5 1.8 %multiply_subtract_fusion.5 = f32[256,256]{1,0:T(8,128)} fusion(f32[256,256]{1,0:T(8,128)} %get-tuple-element.633, f32[256,256]{1,0:T(8,128)} %get-tuple-element.636), kind=kLoop, calls=%fused_computation.53 | loop fusion | flops 262144 | bytes 786432 | tf_op jit(solution)/shard_map/cond/branch_5_fun/sub | solution.py:143
  34.3 5.0 %collective-permute-done.33 = f32[256,256]{1,0:T(8,128)} collective-permute-done((f32[256,256]{1,0:T(8,128)S(1)}, f32[256,256]{1,0:T(8,128)}, u32[]{:S(2)}, u32[]{:S(2)}) %collective-permute-start.33) | collective-permute-done | bytes 262176 | tf_op jit(solution)/shard_map/cond/branch_5_fun/ppermute | solution.py:24
  39.2 1.0 copy.79
  40.2 15.4 %conditional.12 = (f32[256,256]{1,0:T(8,128)}, f32[3072,256]{1,0:T(8,128)}, f32[256,256]{1,0:T(8,128)}) conditional(s32[]{:T(128)} %bitcast.33, (f32[256,256]{1,0:T(8,128)S(1)}, s32[96]{0:T(128)S(1)}, s32[96]{0:T(128)S(1)}, f32[3072,256]{1,0:T(8,128)S(1)}, bf16[128,128,128]{2,1,0:T(8,128)(2,1)}, ...), branch_computations={%region_32.33_spmd, %region_33.34_spmd, %region_34.35_spmd, %regio... | conditional | flops 1208287232 | bytes 14155840 | solution.py:28
  40.9 7.5 %branch_4_fun.5 = (f32[3072,256]{1,0:T(8,128)}, f32[256,256]{1,0:T(8,128)}) custom-call(s32[96]{0:T(128)S(1)} %get-tuple-element.690.slot_ref, s32[96]{0:T(128)S(1)} %get-tuple-element.691.live_ref, f32[3072,256]{1,0:T(8,128)S(1)} %get-tuple-element.692.user_ref, bf16[256,256]{1,0:T(8,128)(2,1)} %convert_element_type.134.panel_ref, ...), custom_call_target="tpu_custom_call", output_to_operand_aliasing={{0}: (12, {})} | custom-call | flops 1207959552 | bytes 11403264 | tf_op jit(solution)/shard_map/cond/branch_4_fun/pallas_call | solution.py:111
  48.4 1.7 %multiply_subtract_fusion.12 = f32[256,256]{1,0:T(8,128)} fusion(f32[256,256]{1,0:T(8,128)S(1)} %get-tuple-element.693, f32[256,256]{1,0:T(8,128)} %get-tuple-element.697), kind=kLoop, calls=%fused_computation.60 | loop fusion | flops 262144 | bytes 786432 | tf_op jit(solution)/shard_map/cond/branch_4_fun/sub | solution.py:143
  50.1 3.5 %collective-permute-done.39 = f32[256,256]{1,0:T(8,128)} collective-permute-done((f32[256,256]{1,0:T(8,128)}, f32[256,256]{1,0:T(8,128)}, u32[]{:S(2)}, u32[]{:S(2)}) %collective-permute-start.39) | collective-permute-done | bytes 262176 | tf_op jit(solution)/shard_map/cond/branch_4_fun/ppermute | solution.py:24
  53.6 1.7 %copy.100 = f32[256,256]{1,0:T(8,128)} copy(f32[256,256]{1,0:T(8,128)} %collective-permute-done.39) | data formatting | bytes 524288 | tf_op jit(solution)/shard_map/cond
  55.6 28.7 %conditional.17 = (f32[256,256]{1,0:T(8,128)}, f32[3072,256]{1,0:T(8,128)}, s32[96]{0:T(128)}, f32[3072,256]{1,0:T(8,128)S(1)}, f32[256,256]{1,0:T(8,128)}, /*index=5*/s32[96]{0:T(128)}) conditional(s32[]{:T(128)} %bitcast.33, (f32[3072,256]{1,0:T(8,128)}, f32[3072,256]{1,0:T(8,128)S(1)}, s32[1,1,128]{2,1,0:T(1,128)S(1)}, ...), branch_computations={%region_40.43_spmd, %region_43.46_spmd, %region_46.49_spmd, %regio... | conditional | flops 1212262400 | bytes 36178956
  57.8 1.6 %convert_element_type.147.panel_ref = bf16[256,256]{1,0:T(8,128)(2,1)} convert(f32[256,256]{1,0:T(8,128)} %get-tuple-element.766) | non-fusion elementwise | flops 65536 | bytes 393216 | tf_op jit(solution)/shard_map/cond/branch_4_fun/convert_element_type | solution.py:141
  60.0 9.7 %collective-permute-done.50 = f32[256,256]{1,0:T(8,128)S(1)} collective-permute-done((f32[256,256]{1,0:T(8,128)}, f32[256,256]{1,0:T(8,128)S(1)}, u32[]{:S(2)}, u32[]{:S(2)}) %collective-permute-start.50) | collective-permute-done | bytes 262176 | tf_op jit(solution)/shard_map/cond/branch_4_fun/ppermute | solution.py:24
  70.4 4.5 %multiply_subtract_fusion.24.user_ref = f32[3072,256]{1,0:T(8,128)} fusion(f32[3072,256]{1,0:T(8,128)S(1)} %get-tuple-element.762, f32[3072,256]{1,0:T(8,128)} %get-tuple-element.763, f32[3072,256]{1,0:T(8,128)S(1)} %collective-permute-done.51), kind=kLoop, calls=%fused_computation.100 | loop fusion | flops 3932160 | bytes 12582912 | tf_op jit(solution)/shard_map/cond/branch_4_fun/sub | solution.py:170
  74.9 7.4 %branch_4_fun.6 = (f32[3072,256]{1,0:T(8,128)S(1)}, f32[256,256]{1,0:T(8,128)}) custom-call(s32[96]{0:T(128)} %broadcast_add_fusion.4.slot_ref, s32[96]{0:T(128)} %convert_element_type.146.live_ref, f32[3072,256]{1,0:T(8,128)} %multiply_subtract_fusion.24.user_ref, bf16[256,256]{1,0:T(8,128)(2,1)} %convert_element_type.147.panel_ref, ...), custom_call_target="tpu_custom_call" | custom-call | flops 1207959552 | bytes 8257536 | tf_op jit(solution)/shard_map/cond/branch_4_fun/pallas_call | solution.py:111
  82.3 1.8 %multiply_subtract_fusion.25 = f32[256,256]{1,0:T(8,128)} fusion(f32[256,256]{1,0:T(8,128)} %get-tuple-element.766, f32[256,256]{1,0:T(8,128)} %get-tuple-element.769), kind=kLoop, calls=%fused_computation.101 | loop fusion | flops 262144 | bytes 786432 | tf_op jit(solution)/shard_map/cond/branch_4_fun/sub | solution.py:143
  84.3 14.8 %conditional.14 = (f32[256,256]{1,0:T(8,128)}, f32[3072,256]{1,0:T(8,128)S(1)}, f32[256,256]{1,0:T(8,128)}, f32[3072,256]{1,0:T(8,128)S(1)}, f32[256,256]{1,0:T(...) conditional(s32[]{:T(128)} %bitcast.32, (f32[256,256]{1,0:T(8,128)}, ...), branch_computations={%region_64.65_spmd, %region_65.66_spmd, %region_66.67_spmd, %regio... | conditional | flops 1208025088 | bytes 20709472 | solution.py:28
  84.3 1.9 %collective-permute-start = (f32[256,256]{1,0:T(8,128)}, f32[256,256]{1,0:T(8,128)}, u32[]{:S(2)}, u32[]{:S(2)}) collective-permute-start(f32[256,256]{1,0:T(8,128)} %get-tuple-element.806), channel_id=1, source_target_pairs={{0,2},{2,0},{4,6},{6,4},{8,10},{10,8},{12,14},{14,12},{1,3},{3,1},... | collective-permute-start | bytes 786440 | tf_op jit(solution)/shard_map/cond/branch_1_fun/ppermute | solution.py:24
  86.2 1.6 %convert_element_type.155.panel_ref = bf16[256,256]{1,0:T(8,128)(2,1)} convert(f32[256,256]{1,0:T(8,128)} %get-tuple-element.1298) | non-fusion elementwise | flops 65536 | bytes 393216 | tf_op jit(solution)/shard_map/cond/branch_1_fun/convert_element_type | solution.py:141
  88.8 7.5 %branch_1_fun.7 = (f32[3072,256]{1,0:T(8,128)S(1)}, f32[256,256]{1,0:T(8,128)}) custom-call(s32[96]{0:T(128)} %get-tuple-element.807.slot_ref, s32[96]{0:T(128)} %get-tuple-element.808.live_ref, f32[3072,256]{1,0:T(8,128)} %get-tuple-element.809.user_ref, bf16[256,256]{1,0:T(8,128)(2,1)} %convert_element_type.155.panel_ref, ...), custom_call_target="tpu_custom_call", output_to_operand_aliasing={{0}: (12, {})} | custom-call | flops 1207959552 | bytes 11403264 | tf_op jit(solution)/shard_map/cond/branch_1_fun/pallas_call | solution.py:111
  96.5 1.7 %copy.165 = f32[256,256]{1,0:T(8,128)} copy(f32[256,256]{1,0:T(8,128)} %collective-permute-done) | data formatting | bytes 524288 | tf_op jit(solution)/shard_map/cond
  99.9 9.7 %conditional.15 = (f32[256,256]{1,0:T(8,128)}, f32[3072,256]{1,0:T(8,128)}, f32[3072,256]{1,0:T(8,128)}, f32[3072,256]{1,0:T(8,128)S(1)}, f32[3072,256]{1,0:T(8,128)S(1)}, /*index=5*/f32[3072,256]{1,0:T(8,128)}) conditional(s32[]{:T(128)} %bitcast.32, (f32[3072,256]{1,0:T(8,128)S(1)}, f32[256,256]{1,0:T(8,128)}, ...), branch_computations={%region_72.73_spmd, %region_73.74_spmd, %region_74.75_spmd, %regio... | conditional | bytes 26738816 | solution.py:28
  100.3 3.8 %copy.234 = f32[3072,256]{1,0:T(8,128)} copy(f32[3072,256]{1,0:T(8,128)} %get-tuple-element.1246) | data formatting | bytes 6291456 | tf_op jit(solution)/shard_map/cond
  104.1 4.8 %collective-permute-done.8 = f32[256,256]{1,0:T(8,128)S(1)} collective-permute-done((f32[256,256]{1,0:T(8,128)}, f32[256,256]{1,0:T(8,128)S(1)}, u32[]{:S(2)}, u32[]{:S(2)}) %collective-permute-start.8) | collective-permute-done | bytes 262176 | tf_op jit(solution)/shard_map/cond/branch_1_fun/ppermute | solution.py:24
  109.5 5.1 %multiply_subtract_fusion.32 = f32[3072,256]{1,0:T(8,128)} fusion(f32[3072,256]{1,0:T(8,128)} %get-tuple-element.936, f32[3072,256]{1,0:T(8,128)S(1)} %get-tuple-element.937, f32[3072,256]{1,0:T(8,128)} %get-tuple-element.938), kind=kLoop, calls=%fused_computation.136 | loop fusion | flops 3932160 | bytes 12582912 | tf_op jit(solution)/shard_map/cond/branch_0_fun/sub | solution.py:170
  114.7 1.9 %pad_maximum_fusion = f32[512,256]{1,0:T(8,128)} fusion(f32[256,256]{1,0:T(8,128)} %get-tuple-element.940, f32[256,256]{1,0:T(8,128)} %get-tuple-element.939), kind=kLoop, calls=%fused_computation.137 | loop fusion | flops 131072 | bytes 1048576 | tf_op jit(solution)/shard_map/concatenate | solution.py:179
  (36 shorter events, 10.3 us)
Async XLA Ops:
  0.6 23.6 %copy-start = (f32[3072,256]{1,0:T(8,128)S(1)}, f32[3072,256]{1,0:T(8,128)}, u32[]{:S(2)}) copy-start(f32[3072,256]{1,0:T(8,128)} %param.54) | copy-start | bytes 9437188
  6.4 17.1 %collective-permute-start.26 = (f32[256,256]{1,0:T(8,128)}, f32[256,256]{1,0:T(8,128)S(1)}, u32[]{:S(2)}, u32[]{:S(2)}) collective-permute-start(f32[256,256]{1,0:T(8,128)} %get-tuple-element.580), channel_id=1, source_target_pairs={{0,10},{2,8},{4,14},{6,12},{8,2},{10,0},{12,6},{14,4},{1,11},{3,9}... | collective-permute-start | bytes 786440 | tf_op jit(solution)/shard_map/cond/branch_5_fun/ppermute | solution.py:24
  24.2 15.0 %collective-permute-start.33 = (f32[256,256]{1,0:T(8,128)S(1)}, f32[256,256]{1,0:T(8,128)}, u32[]{:S(2)}, u32[]{:S(2)}) collective-permute-start(f32[256,256]{1,0:T(8,128)S(1)} %get-tuple-element.629), channel_id=1, source_target_pairs={{0,10},{2,8},{4,14},{6,12},{8,2},{10,0},{12,6},{14,4},{1,11},{3,9}... | collective-permute-start | bytes 786440 | tf_op jit(solution)/shard_map/cond/branch_5_fun/ppermute | solution.py:24
  40.2 15.4 %copy-start.1 = (s32[1,1,128]{2,1,0:T(1,128)S(1)}, s32[1,1,128]{2,1,0:T(1,128)}, u32[]{:S(2)}) copy-start(s32[1,1,128]{2,1,0:T(1,128)} %param.57) | copy-start | bytes 1540
  40.2 15.4 %copy-start.2 = (s32[1,1,2]{2,1,0:T(1,128)S(1)}, s32[1,1,2]{2,1,0:T(1,128)}, u32[]{:S(2)}) copy-start(s32[1,1,2]{2,1,0:T(1,128)} %param.58) | copy-start | bytes 28
  40.2 13.4 %collective-permute-start.39 = (f32[256,256]{1,0:T(8,128)}, f32[256,256]{1,0:T(8,128)}, u32[]{:S(2)}, u32[]{:S(2)}) collective-permute-start(f32[256,256]{1,0:T(8,128)} %get-tuple-element.689), channel_id=1, source_target_pairs={{0,8},{2,10},{4,12},{6,14},{8,0},{10,2},{12,4},{14,6},{1,9},{3,11}... | collective-permute-start | bytes 786440 | tf_op jit(solution)/shard_map/cond/branch_4_fun/ppermute | solution.py:24
  55.6 14.8 %collective-permute-start.51 = (f32[3072,256]{1,0:T(8,128)}, f32[3072,256]{1,0:T(8,128)S(1)}, u32[]{:S(2)}, u32[]{:S(2)}) collective-permute-start(f32[3072,256]{1,0:T(8,128)} %get-tuple-element.763), channel_id=1, source_target_pairs={{0,1},{1,0},{2,3},{3,2},{4,5},{5,4},{6,7},{7,6},{8,9},{9,8},{10,11... | collective-permute-start | bytes 9437192 | tf_op jit(solution)/shard_map/cond/branch_4_fun/ppermute | solution.py:33
  55.7 14.0 %collective-permute-start.50 = (f32[256,256]{1,0:T(8,128)}, f32[256,256]{1,0:T(8,128)S(1)}, u32[]{:S(2)}, u32[]{:S(2)}) collective-permute-start(f32[256,256]{1,0:T(8,128)} %get-tuple-element.761), channel_id=1, source_target_pairs={{0,8},{2,10},{4,12},{6,14},{8,0},{10,2},{12,4},{14,6},{1,9},{3,11}... | collective-permute-start | bytes 786440 | tf_op jit(solution)/shard_map/cond/branch_4_fun/ppermute | solution.py:24
  84.3 12.2 %collective-permute-start = (f32[256,256]{1,0:T(8,128)}, f32[256,256]{1,0:T(8,128)}, u32[]{:S(2)}, u32[]{:S(2)}) collective-permute-start(f32[256,256]{1,0:T(8,128)} %get-tuple-element.806), channel_id=1, source_target_pairs={{0,2},{2,0},{4,6},{6,4},{8,10},{10,8},{12,14},{14,12},{1,3},{3,1},... | collective-permute-start | bytes 786440 | tf_op jit(solution)/shard_map/cond/branch_1_fun/ppermute | solution.py:24
  99.9 9.7 %collective-permute-start.9 = (f32[3072,256]{1,0:T(8,128)S(1)}, f32[3072,256]{1,0:T(8,128)}, u32[]{:S(2)}, u32[]{:S(2)}) collective-permute-start(f32[3072,256]{1,0:T(8,128)S(1)} %get-tuple-element.1248), channel_id=1, source_target_pairs={{0,1},{1,0},{2,3},{3,2},{4,5},{5,4},{6,7},{7,6},{8,9},{9,8},{10,11... | collective-permute-start | bytes 9437192 | tf_op jit(solution)/shard_map/cond/branch_1_fun/ppermute | solution.py:33
  99.9 8.9 %collective-permute-start.8 = (f32[256,256]{1,0:T(8,128)}, f32[256,256]{1,0:T(8,128)S(1)}, u32[]{:S(2)}, u32[]{:S(2)}) collective-permute-start(f32[256,256]{1,0:T(8,128)} %get-tuple-element.872), channel_id=1, source_target_pairs={{0,2},{2,0},{4,6},{6,4},{8,10},{10,8},{12,14},{14,12},{1,3},{3,1},... | collective-permute-start | bytes 786440 | tf_op jit(solution)/shard_map/cond/branch_1_fun/ppermute | solution.py:24

commit v6 on v4

--- a/solution.py
+++ b/solution.py
@@ -9,7 +9,7 @@
 
 LEARNING_RATE = 0.02
 WEIGHT_DECAY = 0.1
-TILES_PER_STEP = 4
+TILES_PER_STEP = 8
 
 
 def moved(value, partner_mask, work):
@@ -21,7 +21,7 @@
             if mask == 0:
                 return held, done
             pairs = [(source, source ^ mask) for source in range(count)]
-            return lax.ppermute(held, "user", pairs), done
+            return lax.optimization_barrier((lax.ppermute(held, "user", pairs), done))
 
         return run
 

time: 111 us -> 98.6 us (0.89)
  the two profiles are of different devices: /device:TPU:0 before, /device:TPU:4 now
where the time goes in v6:
time: 98.6 us; the launch traced here: 98.4 us
  waiting for transfers between devices  38.8 us (39%)
  starting transfers between devices  19.4 us (20%)
  Pallas kernels  16.4 us (17%)
  other arithmetic  12.6 us (13%)
  local copies, waits for them, and re-layouts  7.59 us (8%)
  between operations  3.3 us (3%)
    ppermute x3, waiting for transfers between devices, run(): return lax.optimization_barrier((lax.ppermute(held, 'user', pairs), done))  38.8 us
    ppermute x3, starting transfers between devices, run(): return lax.optimization_barrier((lax.ppermute(held, 'user', pairs), done))  19.3 us
    pallas_call x2, Pallas kernels, local_grads(): pl.pallas_call(functools.partial(grads_kernel, item_tiles), grid_spec=gri...  16.4 us
    sub x2, other arithmetic, user_step(): rows = user_rows - LEARNING_RATE * (grad_total + WEIGHT_DECAY * user_rows)  6.76 us
    unnamed x12, local copies, waits for them, and re-layouts  4.85 us
    sub x2, other arithmetic, local(): panel_now - LEARNING_RATE * (grad_panel + WEIGHT_DECAY * panel_now)  2.63 us
  transfers between devices with their start and end apart: 5, of which 3 were waited for; matrix products, arithmetic and copies ran while one was open for 11% of the time, Pallas kernels for 0%

profile of v6, /device:TPU:4, one launch (start us, length us, event | category | flops | bytes accessed | tf_op | source)
XLA Modules:
  0.0 98.4 jit_solution(10585418345091061782)
XLA Ops:
  0.6 1.0 %copy.82 = f32[512,256]{1,0:T(8,128)S(1)} copy(f32[512,256]{1,0:T(8,128)} %param.31) | data formatting | bytes 1048576
  1.7 1.3 %fusion.32 = (s32[1]{0:T(128)}, s32[1]{0:T(128)}) fusion(s32[2]{0:T(128)} %param.32), kind=kLoop, calls=%fused_computation.129 | loop fusion | bytes 16 | tf_op jit(solution)/shard_map/slice | solution.py:143
  5.6 14.7 %conditional.3 = (f32[512,256]{1,0:T(8,128)S(1)}, s32[96]{0:T(128)S(1)}, s32[96]{0:T(128)S(1)}) conditional(s32[]{:T(128)} %bitcast.34, (s32[1,1,128]{2,1,0:T(1,128)}, s32[1,1,2]{2,1,0:T(1,128)}, f32[512,256]{1,0:T(8,128)S(1)}) %tuple.104, (f32[512,256]{1,0:T(8,128)S(1)}, s32[1,1,128]{2,1,0:T(1,128)}, ...), branch_computations={%region_0.3_spmd, %region_3.6_spmd, %region_6.9_spmd, %region_9.12... | conditional | flops 42976 | bytes 3147972 | solution.py:28
  5.6 2.6 %collective-permute-start.2 = (f32[512,256]{1,0:T(8,128)S(1)}, f32[512,256]{1,0:T(8,128)S(1)}, u32[]{:S(2)}, u32[]{:S(2)}) collective-permute-start(f32[512,256]{1,0:T(8,128)S(1)} %get-tuple-element.273), channel_id=1, source_target_pairs={{0,6},{2,4},{4,2},{6,0},{8,14},{10,12},{12,10},{14,8},{1,7},{3,5},... | collective-permute-start | bytes 1572872 | tf_op jit(solution)/shard_map/cond/branch_3_fun/ppermute | solution.py:24
  8.2 0.6 iota_compare_fusion.7
  8.8 0.7 slice_bitcast_fusion.3
  9.5 0.1 fusion.7
  9.6 0.1 select_reduce_fusion.3
  9.7 10.5 %collective-permute-done.2 = f32[512,256]{1,0:T(8,128)S(1)} collective-permute-done((f32[512,256]{1,0:T(8,128)S(1)}, f32[512,256]{1,0:T(8,128)S(1)}, u32[]{:S(2)}, u32[]{:S(2)}) %collective-permute-start.2) | collective-permute-done | bytes 524320 | tf_op jit(solution)/shard_map/cond/branch_3_fun/ppermute | solution.py:24
  20.3 0.8 copy-done.9
  21.1 0.7 convert_element_type.54.panel_ref
  21.8 8.2 %shard_map.77 = (f32[3072,256]{1,0:T(8,128)S(1)}, f32[512,256]{1,0:T(8,128)}) custom-call(s32[96]{0:T(128)S(1)} %get-tuple-element.383.slot_ref, s32[96]{0:T(128)S(1)} %get-tuple-element.384.live_ref, f32[3072,256]{1,0:T(8,128)} %user_ref.1, bf16[512,256]{1,0:T(8,128)(2,1)} %convert_element_type.54.panel_ref, bf16[128,128,128]{2,1,0:T(8,128)(2,1)} %bitcast.91, ...), custom_call_target="tpu_custom_call" | custom-call | flops 2415919104 | bytes 10223616 | tf_op jit(solution)/shard_map/pallas_call | solution.py:110
  30.1 1.3 %multiply_subtract_fusion.24 = f32[512,256]{1,0:T(8,128)S(1)} fusion(f32[512,256]{1,0:T(8,128)} %copy-done.9, f32[512,256]{1,0:T(8,128)} %get-tuple-element.387), kind=kLoop, calls=%fused_computation.128 | loop fusion | flops 524288 | bytes 1572864 | tf_op jit(solution)/shard_map/sub | solution.py:138
  31.4 17.6 %conditional.4 = (f32[512,256]{1,0:T(8,128)S(1)}, f32[3072,256]{1,0:T(8,128)S(1)}, s32[96]{0:T(128)S(1)}, s32[96]{0:T(128)S(1)}) conditional(s32[]{:T(128)} %bitcast.33, (f32[3072,256]{1,0:T(8,128)S(1)}, f32[3072,256]{1,0:T(8,128)}, s32[1,1,128]{2,1,0:T(1,128)S(1)}, s32[1,1,2]{2,1,0:T(1,128)S(1)}, ...), branch_computations={%region_24.27_spmd, %region_27.30_spmd, %region_30.33_spmd, %regio... | conditional | flops 3975232 | bytes 40897560 | solution.py:28
  31.4 0.1 collective-permute-start.21
  31.5 4.6 %collective-permute-start.20 = (f32[512,256]{1,0:T(8,128)S(1)}, f32[512,256]{1,0:T(8,128)S(1)}, u32[]{:S(2)}, u32[]{:S(2)}) collective-permute-start(f32[512,256]{1,0:T(8,128)S(1)} %get-tuple-element.323), channel_id=1, source_target_pairs={{0,14},{2,12},{4,10},{6,8},{8,6},{10,4},{12,2},{14,0},{1,15},{3,13... | collective-permute-start | bytes 1572872 | tf_op jit(solution)/shard_map/cond/branch_7_fun/ppermute | solution.py:24
  36.1 0.6 slice.101
  36.7 0.6 iota_compare_fusion.31
  37.4 0.1 slice_bitcast_fusion.15
  37.4 0.1 fusion.31
  37.6 0.1 select_reduce_fusion.15
  37.7 3.9 %multiply_subtract_fusion.7 = f32[3072,256]{1,0:T(8,128)S(1)} fusion(f32[3072,256]{1,0:T(8,128)} %get-tuple-element.324, f32[3072,256]{1,0:T(8,128)} %copy-done.7, f32[3072,256]{1,0:T(8,128)S(1)} %collective-permute-done.21), kind=kLoop, calls=%fused_computation.104 | loop fusion | flops 3932160 | bytes 12582912 | tf_op jit(solution)/shard_map/cond/branch_7_fun/sub | solution.py:147
  41.6 7.2 %collective-permute-done.20 = f32[512,256]{1,0:T(8,128)S(1)} collective-permute-done((f32[512,256]{1,0:T(8,128)S(1)}, f32[512,256]{1,0:T(8,128)S(1)}, u32[]{:S(2)}, u32[]{:S(2)}) %collective-permute-start.20) | collective-permute-done | bytes 524320 | tf_op jit(solution)/shard_map/cond/branch_7_fun/ppermute | solution.py:24
  49.0 0.8 copy-done.8
  49.8 0.7 convert_element_type.55.panel_ref
  50.5 8.2 %shard_map.78 = (f32[3072,256]{1,0:T(8,128)}, f32[512,256]{1,0:T(8,128)}) custom-call(s32[96]{0:T(128)S(1)} %get-tuple-element.389.slot_ref, s32[96]{0:T(128)S(1)} %get-tuple-element.390.live_ref, f32[3072,256]{1,0:T(8,128)S(1)} %get-tuple-element.391.user_ref, bf16[512,256]{1,0:T(8,128)(2,1)} %convert_element_type.55.panel_ref, ...), custom_call_target="tpu_custom_call" | custom-call | flops 2415919104 | bytes 10223616 | tf_op jit(solution)/shard_map/pallas_call | solution.py:110
  58.7 37.4 %conditional.5 = (f32[512,256]{1,0:T(8,128)}, f32[3072,256]{1,0:T(8,128)S(1)}) conditional(s32[]{:T(128)} %bitcast.32, (f32[512,256]{1,0:T(8,128)}, f32[512,256]{1,0:T(8,128)}, f32[512,256]{1,0:T(8,128)S(1)}, f32[3072,256]{1,0:T(8,128)}, f32[3072,256]{1,0:T(8,128)S(1)}) %tuple.137, (f32[512,256]{1,0:T(8,128)}, ...), branch_computations={%region_48.49_spmd, %region_49.50_spmd, %region_50.51_spmd, %regio... | conditional | flops 4456448 | bytes 29360224 | solution.py:28
  58.8 1.3 %multiply_subtract_fusion.17 = f32[512,256]{1,0:T(8,128)S(1)} fusion(f32[512,256]{1,0:T(8,128)} %get-tuple-element.348, f32[512,256]{1,0:T(8,128)S(1)} %get-tuple-element.350, f32[512,256]{1,0:T(8,128)} %get-tuple-element.349), kind=kLoop, calls=%fused_computation.121 | loop fusion | flops 524288 | bytes 2097152 | tf_op jit(solution)/shard_map/sub | solution.py:138
  60.2 12.1 %collective-permute-start.29 = (f32[512,256]{1,0:T(8,128)S(1)}, f32[512,256]{1,0:T(8,128)}, u32[]{:S(2)}, u32[]{:S(2)}) collective-permute-start(f32[512,256]{1,0:T(8,128)S(1)} %multiply_subtract_fusion.17), channel_id=1, source_target_pairs={{0,8},{2,10},{4,12},{6,14},{8,0},{10,2},{12,4},{14,6},{1,9},{3,11}... | collective-permute-start | bytes 1572872 | tf_op jit(solution)/shard_map/cond/branch_4_fun/ppermute | solution.py:24
  72.2 2.9 %multiply_subtract_fusion.16 = f32[3072,256]{1,0:T(8,128)S(1)} fusion(f32[3072,256]{1,0:T(8,128)S(1)} %get-tuple-element.351, f32[3072,256]{1,0:T(8,128)} %get-tuple-element.352, f32[3072,256]{1,0:T(8,128)S(1)} %collective-permute-done.30), kind=kLoop, calls=%fused_computation.120 | loop fusion | flops 3932160 | bytes 12582912 | tf_op jit(solution)/shard_map/cond/branch_4_fun/sub | solution.py:147
  75.1 21.0 %collective-permute-done.29 = f32[512,256]{1,0:T(8,128)} collective-permute-done((f32[512,256]{1,0:T(8,128)S(1)}, f32[512,256]{1,0:T(8,128)}, u32[]{:S(2)}, u32[]{:S(2)}) %collective-permute-start.29) | collective-permute-done | bytes 524320 | tf_op jit(solution)/shard_map/cond/branch_4_fun/ppermute | solution.py:24
  96.2 2.2 %copy.83 = f32[512,256]{1,0:T(8,128)} copy(f32[512,256]{1,0:T(8,128)} %get-tuple-element.473) | data formatting | bytes 1048576
  (19 shorter events, 0.2 us)
Async XLA Ops:
  5.6 14.6 %collective-permute-start.2 = (f32[512,256]{1,0:T(8,128)S(1)}, f32[512,256]{1,0:T(8,128)S(1)}, u32[]{:S(2)}, u32[]{:S(2)}) collective-permute-start(f32[512,256]{1,0:T(8,128)S(1)} %get-tuple-element.273), channel_id=1, source_target_pairs={{0,6},{2,4},{4,2},{6,0},{8,14},{10,12},{12,10},{14,8},{1,7},{3,5},... | collective-permute-start | bytes 1572872 | tf_op jit(solution)/shard_map/cond/branch_3_fun/ppermute | solution.py:24
  20.3 0.8 copy-start.9
  21.8 9.5 %copy-start.11 = (s32[1,1,128]{2,1,0:T(1,128)S(1)}, s32[1,1,128]{2,1,0:T(1,128)}, u32[]{:S(2)}) copy-start(s32[1,1,128]{2,1,0:T(1,128)} %param.33) | copy-start | bytes 1540
  21.8 9.5 %copy-start.12 = (s32[1,1,2]{2,1,0:T(1,128)S(1)}, s32[1,1,2]{2,1,0:T(1,128)}, u32[]{:S(2)}) copy-start(s32[1,1,2]{2,1,0:T(1,128)} %param.34) | copy-start | bytes 28
  31.4 6.3 %copy-start.7 = (f32[3072,256]{1,0:T(8,128)}, f32[3072,256]{1,0:T(8,128)S(1)}, u32[]{:S(2)}) copy-start(f32[3072,256]{1,0:T(8,128)S(1)} %get-tuple-element.325) | copy-start | bytes 9437188 | tf_op jit(solution)/shard_map/cond
  31.4 6.2 %collective-permute-start.21 = (f32[3072,256]{1,0:T(8,128)S(1)}, f32[3072,256]{1,0:T(8,128)S(1)}, u32[]{:S(2)}, u32[]{:S(2)}) collective-permute-start(f32[3072,256]{1,0:T(8,128)S(1)} %get-tuple-element.325), channel_id=1, source_target_pairs={{0,1},{1,0},{2,3},{3,2},{4,5},{5,4},{6,7},{7,6},{8,9},{9,8},{10,11... | collective-permute-start | bytes 9437192 | tf_op jit(solution)/shard_map/cond/branch_7_fun/ppermute | solution.py:33
  31.5 17.3 %collective-permute-start.20 = (f32[512,256]{1,0:T(8,128)S(1)}, f32[512,256]{1,0:T(8,128)S(1)}, u32[]{:S(2)}, u32[]{:S(2)}) collective-permute-start(f32[512,256]{1,0:T(8,128)S(1)} %get-tuple-element.323), channel_id=1, source_target_pairs={{0,14},{2,12},{4,10},{6,8},{8,6},{10,4},{12,2},{14,0},{1,15},{3,13... | collective-permute-start | bytes 1572872 | tf_op jit(solution)/shard_map/cond/branch_7_fun/ppermute | solution.py:24
  49.0 0.8 copy-start.8
  58.8 13.5 %collective-permute-start.30 = (f32[3072,256]{1,0:T(8,128)}, f32[3072,256]{1,0:T(8,128)S(1)}, u32[]{:S(2)}, u32[]{:S(2)}) collective-permute-start(f32[3072,256]{1,0:T(8,128)} %get-tuple-element.352), channel_id=1, source_target_pairs={{0,1},{1,0},{2,3},{3,2},{4,5},{5,4},{6,7},{7,6},{8,9},{9,8},{10,11... | collective-permute-start | bytes 9437192 | tf_op jit(solution)/shard_map/cond/branch_4_fun/ppermute | solution.py:33
  60.2 36.0 %collective-permute-start.29 = (f32[512,256]{1,0:T(8,128)S(1)}, f32[512,256]{1,0:T(8,128)}, u32[]{:S(2)}, u32[]{:S(2)}) collective-permute-start(f32[512,256]{1,0:T(8,128)S(1)} %multiply_subtract_fusion.17), channel_id=1, source_target_pairs={{0,8},{2,10},{4,12},{6,14},{8,0},{10,2},{12,4},{14,6},{1,9},{3,11}... | collective-permute-start | bytes 1572872 | tf_op jit(solution)/shard_map/cond/branch_4_fun/ppermute | solution.py:24
  96.2 2.2 %copy-start.10 = (f32[3072,256]{1,0:T(8,128)}, f32[3072,256]{1,0:T(8,128)S(1)}, u32[]{:S(2)}) copy-start(f32[3072,256]{1,0:T(8,128)S(1)} %get-tuple-element.472) | copy-start | bytes 9437188

commit v7 on v6

--- a/solution.py
+++ b/solution.py
@@ -12,7 +12,7 @@
 TILES_PER_STEP = 8
 
 
-def moved(value, partner_mask, work):
+def moved(value, partner_mask, work, may_stay):
     count = lax.axis_size("user")
 
     def branch(mask):
@@ -25,7 +25,9 @@
 
         return run
 
-    return lax.switch(partner_mask, [branch(mask) for mask in range(count)], value)
+    if may_stay:
+        return lax.switch(partner_mask, [branch(mask) for mask in range(count)], value)
+    return lax.switch(partner_mask - 1, [branch(mask) for mask in range(1, count)], value)
 
 
 def item_sum(value):
@@ -36,16 +38,17 @@
 
 def grads_kernel(item_tiles, slot_ref, live_ref, user_ref, panel_ref, *rest):
     block_refs = rest[: TILES_PER_STEP * item_tiles]
-    grad_user_ref, grad_panel_ref = rest[TILES_PER_STEP * item_tiles :]
+    grad_user_ref, grad_panel_ref, panel_bf_ref = rest[TILES_PER_STEP * item_tiles :]
     step = pl.program_id(0)
     tile_size = block_refs[0].shape[-1]
 
     @pl.when(step == 0)
     def _():
         grad_panel_ref[...] = jnp.zeros_like(grad_panel_ref)
+        panel_bf_ref[...] = panel_ref[...].astype(jnp.bfloat16)
 
     user_bf = user_ref[...].astype(jnp.bfloat16)
-    panel_bf = panel_ref[...]
+    panel_bf = panel_bf_ref[...]
     scores = lax.dot_general(
         user_bf, panel_bf, (((1,), (1,)), ((), ())), preferred_element_type=jnp.float32
     )
@@ -104,9 +107,10 @@
             pl.BlockSpec((rows, rank), lambda step, slot_ref, live_ref: (step, 0)),
             pl.BlockSpec((columns, rank), lambda step, slot_ref, live_ref: (0, 0)),
         ],
+        scratch_shapes=[pltpu.VMEM((columns, rank), jnp.bfloat16)],
     )
     flops = 3 * 2 * code_count * tile_size * tile_size * rank
-    moved_bytes = user_rows.size * 8 + panel_bf.size * 6 + code_count * tile_size * tile_size * 2
+    moved_bytes = user_rows.size * 8 + panel_bf.size * 8 + code_count * tile_size * tile_size * 2
     return pl.pallas_call(
         functools.partial(grads_kernel, item_tiles),
         grid_spec=grid_spec,
@@ -132,9 +136,9 @@
         return slot_tables(codes, count, stratum * slot_count, code_count)
 
     user_rows = user_factors
-    panel_now, ready = moved(item_factors, stratum_masks[0], lambda: tables(0))
+    panel_now, ready = moved(item_factors, stratum_masks[0], lambda: tables(0), False)
     for stratum in range(stratum_total):
-        grad_user, grad_panel = local_grads(user_rows, panel_now.astype(jnp.bfloat16), ready, all_blocks)
+        grad_user, grad_panel = local_grads(user_rows, panel_now, ready, all_blocks)
         panel_next = panel_now - LEARNING_RATE * (grad_panel + WEIGHT_DECAY * panel_now)
         last = stratum + 1 == stratum_total
         if last:
@@ -147,7 +151,7 @@
             rows = user_rows - LEARNING_RATE * (grad_total + WEIGHT_DECAY * user_rows)
             return rows, (None if last else tables(stratum + 1))
 
-        panel_now, (user_rows, ready) = moved(panel_next, step_mask, user_step)
+        panel_now, (user_rows, ready) = moved(panel_next, step_mask, user_step, not last)
     return (user_rows, panel_now)
 
 

time: 98.6 us -> 96.4 us (0.978)
  the two profiles are of different devices: /device:TPU:4 before, /device:TPU:9 now
where the time goes in v7:
time: 96.4 us; the launch traced here: 94.8 us
  waiting for transfers between devices  49.9 us (52%)
  Pallas kernels  16.7 us (17%)
  other arithmetic  11.8 us (12%)
  starting transfers between devices  6.98 us (7%)
  local copies, waits for them, and re-layouts  5.72 us (6%)
  between operations  3.29 us (3%)
    ppermute x3, waiting for transfers between devices, run(): return lax.optimization_barrier((lax.ppermute(held, 'user', pairs), done))  45.5 us
    pallas_call x2, Pallas kernels, local_grads(): pl.pallas_call(functools.partial(grads_kernel, item_tiles), grid_spec=gri...  16.7 us
    sub x2, other arithmetic, user_step(): rows = user_rows - LEARNING_RATE * (grad_total + WEIGHT_DECAY * user_rows)  7.46 us
    ppermute x3, starting transfers between devices, run(): return lax.optimization_barrier((lax.ppermute(held, 'user', pairs), done))  4.66 us
    ppermute x2, waiting for transfers between devices, item_sum(): return value + lax.ppermute(value, 'item', [(0, 1), (1, 0)])  4.41 us
    unnamed x11, local copies, waits for them, and re-layouts  3.03 us
    sub x2, other arithmetic, local(): panel_now - LEARNING_RATE * (grad_panel + WEIGHT_DECAY * panel_now)  2.62 us
    ppermute x2, starting transfers between devices, item_sum(): return value + lax.ppermute(value, 'item', [(0, 1), (1, 0)])  2.32 us
  transfers between devices with their start and end apart: 5, of which 5 were waited for; matrix products, arithmetic and copies ran while one was open for 12% of the time, Pallas kernels for 0%

profile of v7, /device:TPU:9, one launch (start us, length us, event | category | flops | bytes accessed | tf_op | source)
XLA Modules:
  0.0 94.8 jit_solution(17412203165478333906)
XLA Ops:
  0.6 1.3 %fusion.30 = (s32[1]{0:T(128)}, s32[1]{0:T(128)}) fusion(s32[2]{0:T(128)} %param.30), kind=kLoop, calls=%fused_computation.121 | loop fusion | bytes 16 | tf_op jit(solution)/shard_map/slice | solution.py:147
  4.5 14.1 %conditional.3 = (f32[512,256]{1,0:T(8,128)}, s32[96]{0:T(128)S(1)}, s32[96]{0:T(128)S(1)}) conditional(s32[]{:T(128)} %bitcast.32, (f32[512,256]{1,0:T(8,128)}, s32[1,1,128]{2,1,0:T(1,128)}, s32[1,1,2]{2,1,0:T(1,128)}) %tuple.96, (f32[512,256]{1,0:T(8,128)}, s32[1,1,128]{2,1,0:T(1,128)}, ...), branch_computations={%region_0.3_spmd, %region_3.6_spmd, %region_6.9_spmd, %region_9.12... | conditional | flops 42976 | bytes 2099396 | solution.py:30
  4.6 1.2 %collective-permute-start.2 = (f32[512,256]{1,0:T(8,128)}, f32[512,256]{1,0:T(8,128)}, u32[]{:S(2)}, u32[]{:S(2)}) collective-permute-start(f32[512,256]{1,0:T(8,128)} %get-tuple-element.247), channel_id=1, source_target_pairs={{0,6},{2,4},{4,2},{6,0},{8,14},{10,12},{12,10},{14,8},{1,7},{3,5},... | collective-permute-start | bytes 1572872 | tf_op jit(solution)/shard_map/cond/branch_2_fun/ppermute | solution.py:24
  5.7 0.6 iota_compare_fusion.5
  6.4 0.7 slice_bitcast_fusion.2
  7.1 0.1 fusion.5
  7.2 0.1 select_reduce_fusion.2
  7.3 11.4 %collective-permute-done.2 = f32[512,256]{1,0:T(8,128)} collective-permute-done((f32[512,256]{1,0:T(8,128)}, f32[512,256]{1,0:T(8,128)}, u32[]{:S(2)}, u32[]{:S(2)}) %collective-permute-start.2) | collective-permute-done | bytes 524320 | tf_op jit(solution)/shard_map/cond/branch_2_fun/ppermute | solution.py:24
  18.7 8.6 %shard_map.77 = (f32[3072,256]{1,0:T(8,128)}, f32[512,256]{1,0:T(8,128)}) custom-call(s32[96]{0:T(128)S(1)} %get-tuple-element.352.slot_ref, s32[96]{0:T(128)S(1)} %get-tuple-element.353.live_ref, f32[3072,256]{1,0:T(8,128)} %user_ref.1, f32[512,256]{1,0:T(8,128)} %get-tuple-element.354.panel_ref, bf16[128,128,128]{2,1,0:T(8,128)(2,1)} %bitcast.87, ...), custom_call_target="tpu_custom_call" | custom-call | flops 2415919104 | bytes 10485760 | tf_op jit(solution)/shard_map/pallas_call | solution.py:114
  27.3 1.3 %multiply_subtract_fusion.22 = f32[512,256]{1,0:T(8,128)S(1)} fusion(f32[512,256]{1,0:T(8,128)} %get-tuple-element.354.panel_ref, f32[512,256]{1,0:T(8,128)} %get-tuple-element.356), kind=kLoop, calls=%fused_computation.120 | loop fusion | flops 524288 | bytes 1572864 | tf_op jit(solution)/shard_map/sub | solution.py:142
  28.6 27.9 %conditional.4 = (f32[512,256]{1,0:T(8,128)S(1)}, f32[3072,256]{1,0:T(8,128)}, s32[96]{0:T(128)S(1)}, s32[96]{0:T(128)S(1)}) conditional(s32[]{:T(128)} %bitcast.31, (f32[3072,256]{1,0:T(8,128)}, f32[3072,256]{1,0:T(8,128)S(1)}, s32[1,1,128]{2,1,0:T(1,128)S(1)}, s32[1,1,2]{2,1,0:T(1,128)S(1)}, ...), branch_computations={%region_21.24_spmd, %region_24.27_spmd, %region_27.30_spmd, %regio... | conditional | flops 3975232 | bytes 28314620 | solution.py:29
  28.6 1.5 %collective-permute-start.17 = (f32[3072,256]{1,0:T(8,128)}, f32[3072,256]{1,0:T(8,128)S(1)}, u32[]{:S(2)}, u32[]{:S(2)}) collective-permute-start(f32[3072,256]{1,0:T(8,128)} %get-tuple-element.289), channel_id=1, source_target_pairs={{0,1},{1,0},{2,3},{3,2},{4,5},{5,4},{6,7},{7,6},{8,9},{9,8},{10,11... | collective-permute-start | bytes 9437192 | tf_op jit(solution)/shard_map/cond/branch_5_fun/ppermute | solution.py:35
  30.2 3.4 %collective-permute-start.16 = (f32[512,256]{1,0:T(8,128)S(1)}, f32[512,256]{1,0:T(8,128)S(1)}, u32[]{:S(2)}, u32[]{:S(2)}) collective-permute-start(f32[512,256]{1,0:T(8,128)S(1)} %get-tuple-element.287), channel_id=1, source_target_pairs={{0,10},{2,8},{4,14},{6,12},{8,2},{10,0},{12,6},{14,4},{1,11},{3,9}... | collective-permute-start | bytes 1572872 | tf_op jit(solution)/shard_map/cond/branch_5_fun/ppermute | solution.py:24
  33.6 0.6 slice.91
  34.2 0.6 iota_compare_fusion.25
  34.8 0.1 slice_bitcast_fusion.12
  34.9 0.1 fusion.25
  35.0 0.1 select_reduce_fusion.12
  35.1 0.5 collective-permute-done.17
  35.7 4.6 %multiply_subtract_fusion.5 = f32[3072,256]{1,0:T(8,128)} fusion(f32[3072,256]{1,0:T(8,128)S(1)} %get-tuple-element.288, f32[3072,256]{1,0:T(8,128)} %get-tuple-element.289, f32[3072,256]{1,0:T(8,128)S(1)} %collective-permute-done.17), kind=kLoop, calls=%fused_computation.82 | loop fusion | flops 3932160 | bytes 12582912 | tf_op jit(solution)/shard_map/cond/branch_5_fun/sub | solution.py:151
  40.2 16.1 %collective-permute-done.16 = f32[512,256]{1,0:T(8,128)S(1)} collective-permute-done((f32[512,256]{1,0:T(8,128)S(1)}, f32[512,256]{1,0:T(8,128)S(1)}, u32[]{:S(2)}, u32[]{:S(2)}) %collective-permute-start.16) | collective-permute-done | bytes 524320 | tf_op jit(solution)/shard_map/cond/branch_5_fun/ppermute | solution.py:24
  56.5 0.0 copy-start.1
  56.5 0.8 copy-done.1
  57.3 8.1 %shard_map.78 = (f32[3072,256]{1,0:T(8,128)S(1)}, f32[512,256]{1,0:T(8,128)}) custom-call(s32[96]{0:T(128)S(1)} %get-tuple-element.358.slot_ref, s32[96]{0:T(128)S(1)} %get-tuple-element.359.live_ref, f32[3072,256]{1,0:T(8,128)} %get-tuple-element.360.user_ref, f32[512,256]{1,0:T(8,128)} %copy-done.1, bf16[128,128,128]{2,1,0:T(8,128)(2,1)} %bitcast.88, ...), custom_call_target="tpu_custom_call" | custom-call | flops 2415919104 | bytes 10485760 | tf_op jit(solution)/shard_map/pallas_call | solution.py:114
  65.4 27.1 %conditional.5 = (f32[512,256]{1,0:T(8,128)}, f32[3072,256]{1,0:T(8,128)S(1)}) conditional(s32[]{:T(128)} %bitcast.30, (f32[512,256]{1,0:T(8,128)}, f32[512,256]{1,0:T(8,128)}, f32[512,256]{1,0:T(8,128)S(1)}, f32[3072,256]{1,0:T(8,128)S(1)}, f32[3072,256]{1,0:T(8,128)}) %tuple.134, (f32[512,256]{1,0:T(8,128)}, ...), branch_computations={%region_45.46_spmd, %region_46.47_spmd, %region_47.48_spmd, %regio... | conditional | flops 4456448 | bytes 29360224 | solution.py:30
  65.5 0.8 collective-permute-start.33
  66.3 1.3 %multiply_subtract_fusion.19 = f32[512,256]{1,0:T(8,128)S(1)} fusion(f32[512,256]{1,0:T(8,128)} %get-tuple-element.327, f32[512,256]{1,0:T(8,128)S(1)} %get-tuple-element.329, f32[512,256]{1,0:T(8,128)} %get-tuple-element.328), kind=kLoop, calls=%fused_computation.117 | loop fusion | flops 524288 | bytes 2097152 | tf_op jit(solution)/shard_map/sub | solution.py:142
  67.6 0.1 collective-permute-start.32
  67.7 3.9 %collective-permute-done.33 = f32[3072,256]{1,0:T(8,128)S(1)} collective-permute-done((f32[3072,256]{1,0:T(8,128)S(1)}, f32[3072,256]{1,0:T(8,128)S(1)}, u32[]{:S(2)}, u32[]{:S(2)}) %collective-permute-start.33) | collective-permute-done | bytes 3145760 | tf_op jit(solution)/shard_map/cond/branch_5_fun/ppermute | solution.py:35
  71.6 2.9 %multiply_subtract_fusion.18 = f32[3072,256]{1,0:T(8,128)S(1)} fusion(f32[3072,256]{1,0:T(8,128)} %get-tuple-element.330, f32[3072,256]{1,0:T(8,128)S(1)} %get-tuple-element.331, f32[3072,256]{1,0:T(8,128)S(1)} %collective-permute-done.33), kind=kLoop, calls=%fused_computation.116 | loop fusion | flops 3932160 | bytes 12582912 | tf_op jit(solution)/shard_map/cond/branch_5_fun/sub | solution.py:151
  74.5 18.1 %collective-permute-done.32 = f32[512,256]{1,0:T(8,128)} collective-permute-done((f32[512,256]{1,0:T(8,128)S(1)}, f32[512,256]{1,0:T(8,128)}, u32[]{:S(2)}, u32[]{:S(2)}) %collective-permute-start.32) | collective-permute-done | bytes 524320 | tf_op jit(solution)/shard_map/cond/branch_5_fun/ppermute | solution.py:24
  92.6 2.2 %copy.76 = f32[512,256]{1,0:T(8,128)} copy(f32[512,256]{1,0:T(8,128)} %get-tuple-element.437) | data formatting | bytes 1048576
  (13 shorter events, 0.1 us)
Async XLA Ops:
  4.6 14.1 %collective-permute-start.2 = (f32[512,256]{1,0:T(8,128)}, f32[512,256]{1,0:T(8,128)}, u32[]{:S(2)}, u32[]{:S(2)}) collective-permute-start(f32[512,256]{1,0:T(8,128)} %get-tuple-element.247), channel_id=1, source_target_pairs={{0,6},{2,4},{4,2},{6,0},{8,14},{10,12},{12,10},{14,8},{1,7},{3,5},... | collective-permute-start | bytes 1572872 | tf_op jit(solution)/shard_map/cond/branch_2_fun/ppermute | solution.py:24
  18.6 9.9 %copy-start = (f32[3072,256]{1,0:T(8,128)S(1)}, f32[3072,256]{1,0:T(8,128)}, u32[]{:S(2)}) copy-start(f32[3072,256]{1,0:T(8,128)} %user_ref.1) | copy-start | bytes 9437188
  18.6 9.9 %copy-start.3 = (s32[1,1,128]{2,1,0:T(1,128)S(1)}, s32[1,1,128]{2,1,0:T(1,128)}, u32[]{:S(2)}) copy-start(s32[1,1,128]{2,1,0:T(1,128)} %param.31) | copy-start | bytes 1540
  18.7 9.9 %copy-start.4 = (s32[1,1,2]{2,1,0:T(1,128)S(1)}, s32[1,1,2]{2,1,0:T(1,128)}, u32[]{:S(2)}) copy-start(s32[1,1,2]{2,1,0:T(1,128)} %param.32) | copy-start | bytes 28
  28.6 7.0 %collective-permute-start.17 = (f32[3072,256]{1,0:T(8,128)}, f32[3072,256]{1,0:T(8,128)S(1)}, u32[]{:S(2)}, u32[]{:S(2)}) collective-permute-start(f32[3072,256]{1,0:T(8,128)} %get-tuple-element.289), channel_id=1, source_target_pairs={{0,1},{1,0},{2,3},{3,2},{4,5},{5,4},{6,7},{7,6},{8,9},{9,8},{10,11... | collective-permute-start | bytes 9437192 | tf_op jit(solution)/shard_map/cond/branch_5_fun/ppermute | solution.py:35
  30.2 26.1 %collective-permute-start.16 = (f32[512,256]{1,0:T(8,128)S(1)}, f32[512,256]{1,0:T(8,128)S(1)}, u32[]{:S(2)}, u32[]{:S(2)}) collective-permute-start(f32[512,256]{1,0:T(8,128)S(1)} %get-tuple-element.287), channel_id=1, source_target_pairs={{0,10},{2,8},{4,14},{6,12},{8,2},{10,0},{12,6},{14,4},{1,11},{3,9}... | collective-permute-start | bytes 1572872 | tf_op jit(solution)/shard_map/cond/branch_5_fun/ppermute | solution.py:24
  56.5 0.8 copy-start.1
  65.5 6.1 %collective-permute-start.33 = (f32[3072,256]{1,0:T(8,128)S(1)}, f32[3072,256]{1,0:T(8,128)S(1)}, u32[]{:S(2)}, u32[]{:S(2)}) collective-permute-start(f32[3072,256]{1,0:T(8,128)S(1)} %get-tuple-element.331), channel_id=1, source_target_pairs={{0,1},{1,0},{2,3},{3,2},{4,5},{5,4},{6,7},{7,6},{8,9},{9,8},{10,11... | collective-permute-start | bytes 9437192 | tf_op jit(solution)/shard_map/cond/branch_5_fun/ppermute | solution.py:35
  67.6 24.9 %collective-permute-start.32 = (f32[512,256]{1,0:T(8,128)S(1)}, f32[512,256]{1,0:T(8,128)}, u32[]{:S(2)}, u32[]{:S(2)}) collective-permute-start(f32[512,256]{1,0:T(8,128)S(1)} %multiply_subtract_fusion.19), channel_id=1, source_target_pairs={{0,12},{2,14},{4,8},{6,10},{8,4},{10,6},{12,0},{14,2},{1,13},{3,15... | collective-permute-start | bytes 1572872 | tf_op jit(solution)/shard_map/cond/branch_5_fun/ppermute | solution.py:24
  92.6 2.2 %copy-start.2 = (f32[3072,256]{1,0:T(8,128)}, f32[3072,256]{1,0:T(8,128)S(1)}, u32[]{:S(2)}) copy-start(f32[3072,256]{1,0:T(8,128)S(1)} %get-tuple-element.436) | copy-start | bytes 9437188
